TPU v7x, 256 devices: a whole 4x4x8 slice. The times are simulated.
256 devices in a mesh: dp: 32 (over x, y, z_lo), tensor: 8 (over z_hi, core).
Axes of the slice: x: 4, y: 4, z: 8 (z_hi: 4, z_lo: 2; z = z_hi * 2 + z_lo), core: 2. Of those that a mesh axis runs over, the one named last changes fastest.
Arguments:
- arrivals: bfloat16 [32768, 2048], P('dp', 'tensor')
- deal: int32 [32, 32], P('dp'), may hold values from 0 to 1023, as said below
- seg_ids: int32 [32, 1024], P('dp'), may hold values from 0 to 7, never falling along the last dimension, each value on 1 to 512 neighbouring positions
- page_table: int32 [32, 8], P('dp'), may hold values from 0 to 7, each once within a row
- attn_gain: float32 [2048], replicated, may hold values from 0.1 to 1.9
- w_query: bfloat16 [2048, 1024], P(None, 'tensor'), may hold values from -0.125 to 0.125
- w_keyval: bfloat16 [2048, 512], replicated, may hold values from -0.125 to 0.125
- query_gain: float32 [64], replicated, may hold values from 0.1 to 1.9
- key_gain: float32 [64], replicated, may hold values from 0.1 to 1.9
- w_out: bfloat16 [1024, 2048], P('tensor'), may hold values from -0.1875 to 0.1875
- ffn_gain: float32 [2048], replicated, may hold values from 0.1 to 1.9
- w_gate: bfloat16 [2048, 5120], P(None, 'tensor'), may hold values from -0.125 to 0.125
- w_up: bfloat16 [2048, 5120], P(None, 'tensor'), may hold values from -0.125 to 0.125
- w_down: bfloat16 [5120, 2048], P('tensor'), may hold values from -0.078125 to 0.078125
Outputs:
- result: bfloat16 [32768, 2048], P('dp', 'tensor')
- kv_pages: bfloat16 [256, 128, 512], P('dp', None, 'tensor')
Inputs may be any that keep to these rules, and one draw needn't show every extreme that they name: deal[s, k] = g * 32 + j sends unit k of arrival block s to unit j of group g; every value occurs once; the units of one arrival block go to exactly 16 groups, 2 units to each. `seg_ids`: each row never falls; one prompt is one run of equal numbers. `page_table`: each row holds every page number once.
All inputs are finite; a program needn't handle non-finite values.
Results may differ from a plain program's by a relative error of at most 0.019.
Values may be sent and summed in bfloat16 or wider, within the bound.
No kernel may reach another device: no remote copies, remote signals or barrier semaphores. Data moves between devices by JAX's collectives and lax.ppermute only.
A program may use at most 128 MiB of HBM per device.

v0:
```python
import math

import jax
import jax.numpy as jnp
from jax import lax
from jax.sharding import PartitionSpec as P

HEAD = 64
KVH = 4
MOST = 2
PAGE = 128


EPS = 1e-06
THETA = 10000.0
BLOCK_ROWS = 512


def rms_scale(values, gain):
    values = values.astype(jnp.float32)
    mean_sq = jnp.mean(values * values, axis=-1, keepdims=True)
    return values * lax.rsqrt(mean_sq + EPS) * gain


def rope_tables(positions, width):
    half = width // 2
    inverse = THETA ** (-jnp.arange(half, dtype=jnp.float32) * 2.0 / width)
    angles = positions.astype(jnp.float32)[:, None] * inverse[None, :]
    return (jnp.cos(angles), jnp.sin(angles))


def rotate(values, cosine, sine):
    half = values.shape[-1] // 2
    first = values[..., :half]
    second = values[..., half:]
    cos_b = cosine[:, None, :]
    sin_b = sine[:, None, :]
    return jnp.concatenate(
        [first * cos_b - second * sin_b, second * cos_b + first * sin_b], axis=-1
    )


def segment_starts(seg_row):
    count = seg_row.shape[0]
    index = jnp.arange(count, dtype=jnp.int32)
    prior = jnp.concatenate([seg_row[:1] - 1, seg_row[:-1]])
    marks = jnp.where(seg_row != prior, index, 0)
    return lax.cummax(marks, axis=0)


def on_device(
    arrivals,
    deal,
    seg_ids,
    page_table,
    attn_gain,
    w_query,
    w_keyval,
    query_gain,
    key_gain,
    w_out,
    ffn_gain,
    w_gate,
    w_up,
    w_down,
):
    groups = lax.axis_size("dp")
    shards = lax.axis_size("tensor")
    tensor_rank = lax.axis_index("tensor")
    tok_grp = arrivals.shape[0]
    feat_part = arrivals.shape[1]
    units = deal.shape[1]
    unit_rows = tok_grp // units
    slot_count = groups * MOST
    width = unit_rows * feat_part
    dest_row = deal[0]
    target = dest_row // units
    position = dest_row % units
    unit_index = jnp.arange(units, dtype=jnp.int32)
    earlier = unit_index[:, None] > unit_index[None, :]
    same_target = target[:, None] == target[None, :]
    rank = jnp.sum(jnp.logical_and(earlier, same_target), axis=1)
    slot = target * MOST + rank
    send_hot = slot[None, :] == jnp.arange(slot_count, dtype=jnp.int32)[:, None]
    filled = jnp.any(send_hot, axis=1)
    slot_pos = jnp.where(filled, jnp.sum(jnp.where(send_hot, position[None, :], 0), axis=1), -1)
    send_matrix = send_hot.astype(jnp.bfloat16)
    packed = jnp.dot(
        send_matrix, arrivals.reshape(units, width), preferred_element_type=jnp.float32
    ).astype(jnp.bfloat16)
    received, recv_pos = (
        lax.all_to_all(
            packed.reshape(groups, MOST, width), "dp", split_axis=0, concat_axis=0, tiled=True
        ),
        lax.all_to_all(
            slot_pos.reshape(groups, MOST), "dp", split_axis=0, concat_axis=0, tiled=True
        ),
    )
    recv_matrix = (recv_pos.reshape(-1)[None, :] == unit_index[:, None]).astype(jnp.bfloat16)
    grouped = jnp.dot(
        recv_matrix, received.reshape(slot_count, width), preferred_element_type=jnp.float32
    ).astype(jnp.bfloat16)
    grouped = grouped.reshape(tok_grp, feat_part)
    full = lax.all_gather(grouped, "tensor", axis=1, tiled=True)
    normed = rms_scale(full, attn_gain).astype(jnp.bfloat16)
    seg_row = seg_ids[0]
    starts = segment_starts(seg_row)
    index = jnp.arange(tok_grp, dtype=jnp.int32)
    cosine, sine = rope_tables(index - starts, HEAD)
    q_heads = w_query.shape[1] // HEAD
    q_raw = jnp.dot(normed, w_query, preferred_element_type=jnp.float32).reshape(
        tok_grp, q_heads, HEAD
    )
    queries = rotate(rms_scale(q_raw, query_gain), cosine, sine).astype(jnp.bfloat16)
    kv_heads = max(1, KVH // shards)
    kv_first = tensor_rank * KVH // shards
    kv_weight = lax.dynamic_slice_in_dim(w_keyval, kv_first * 2 * HEAD, kv_heads * 2 * HEAD, 1)
    kv_raw = jnp.dot(normed, kv_weight, preferred_element_type=jnp.float32).reshape(
        tok_grp, kv_heads, 2, HEAD
    )
    keys = rotate(rms_scale(kv_raw[:, :, 0], key_gain), cosine, sine).astype(jnp.bfloat16)
    values = kv_raw[:, :, 1].astype(jnp.bfloat16)
    stacked = jnp.stack([keys, values], axis=2).reshape(tok_grp, kv_heads * 2 * HEAD)
    cache_cols = 2 * KVH * HEAD // shards
    offset = tensor_rank * cache_cols - kv_first * 2 * HEAD
    own_cache = lax.dynamic_slice_in_dim(stacked, offset, cache_cols, 1)
    pages = own_cache.reshape(tok_grp // PAGE, PAGE, cache_cols)
    kv_pages = jnp.zeros_like(pages).at[page_table[0]].set(pages)
    share = q_heads // kv_heads
    grouped_q = queries.reshape(tok_grp, kv_heads, share, HEAD)
    scale = 1.0 / math.sqrt(HEAD)
    block = min(BLOCK_ROWS, tok_grp)
    outputs = []
    for first in range(0, tok_grp, block):
        last = first + block
        scores = (
            jnp.einsum(
                "ikgd,jkd->kgij",
                grouped_q[first:last],
                keys[:last],
                preferred_element_type=jnp.float32,
            )
            * scale
        )
        query_rows = index[first:last]
        allowed = jnp.logical_and(
            query_rows[:, None] >= index[None, :last],
            starts[first:last][:, None] <= index[None, :last],
        )
        weights = jnp.where(allowed, jnp.exp(scores), 0.0)
        probs = (weights / jnp.sum(weights, axis=-1, keepdims=True)).astype(jnp.bfloat16)
        mixed = jnp.einsum(
            "kgij,jkd->ikgd", probs, values[:last], preferred_element_type=jnp.float32
        )
        outputs.append(mixed.astype(jnp.bfloat16).reshape(block, q_heads * HEAD))
    attended = jnp.concatenate(outputs, axis=0)
    attn_sum = lax.psum(
        jnp.dot(attended, w_out, preferred_element_type=jnp.float32).astype(jnp.bfloat16), "tensor"
    ).astype(jnp.float32)
    middle = (full.astype(jnp.float32) + attn_sum).astype(jnp.bfloat16)
    ffn_in = rms_scale(middle, ffn_gain).astype(jnp.bfloat16)
    gate = jnp.dot(ffn_in, w_gate, preferred_element_type=jnp.float32)
    upper = jnp.dot(ffn_in, w_up, preferred_element_type=jnp.float32)
    hidden = (jax.nn.silu(gate) * upper).astype(jnp.bfloat16)
    ffn_part = lax.psum_scatter(
        jnp.dot(hidden, w_down, preferred_element_type=jnp.float32).astype(jnp.bfloat16),
        "tensor",
        scatter_dimension=1,
        tiled=True,
    ).astype(jnp.float32)
    own_cols = lax.dynamic_slice_in_dim(middle, tensor_rank * feat_part, feat_part, 1)
    combined = (own_cols.astype(jnp.float32) + ffn_part).astype(jnp.bfloat16)
    back = jnp.dot(
        recv_matrix.T, combined.reshape(units, width), preferred_element_type=jnp.float32
    ).astype(jnp.bfloat16)
    returned = lax.all_to_all(
        back.reshape(groups, MOST, width), "dp", split_axis=0, concat_axis=0, tiled=True
    )
    result = jnp.dot(
        send_matrix.T, returned.reshape(slot_count, width), preferred_element_type=jnp.float32
    ).astype(jnp.bfloat16)
    return (result.reshape(tok_grp, feat_part), kv_pages)


def solution(mesh):
    return jax.shard_map(
        on_device,
        mesh=mesh,
        in_specs=(
            P("dp", "tensor"),
            P("dp", None),
            P("dp", None),
            P("dp", None),
            P(),
            P(None, "tensor"),
            P(),
            P(),
            P(),
            P("tensor", None),
            P(),
            P(None, "tensor"),
            P(None, "tensor"),
            P("tensor", None),
        ),
        out_specs=(P("dp", "tensor"), P("dp", None, "tensor")),
        check_vma=False,
    )
```

profile of v0, /device:TPU:65, one launch (start us, length us, event | category | flops | bytes accessed | tf_op | source)
XLA Modules:
  0.0 368.1 jit_solution(12057154090771228152)
XLA Ops:
  9.8 8.4 %all-to-all-start = ((s32[32,1,2]{2,1,0:T(1,128)}), s32[32,1,2]{2,1,0:T(1,128)S(1)}, u32[]{:S(2)}, u32[]{:S(2)}) async-start(s32[32,1,2]{2,1,0:T(1,128)} %bitcast.5), calls=%async_computation | async-start | bytes 32768 | tf_op jit(solution)/shard_map/all_to_all | solution.py:95
  19.5 1.5 convolution_convert_fusion.1
  21.0 2.5 reshape.502
  23.5 1.7 all-to-all-done
  25.2 6.3 %all-to-all-start.1 = ((bf16[32,2,8192]{2,1,0:T(2,128)(2,1)}), bf16[32,2,8192]{2,1,0:T(2,128)(2,1)}, u32[]{:S(2)}, u32[]{:S(2)}) async-start(bf16[32,2,8192]{2,1,0:T(2,128)(2,1)} %reshape.502), calls=%async_computation.1 | async-start | bytes 2097152 | tf_op jit(solution)/shard_map/all_to_all | solution.py:92
  32.9 14.9 %all-to-all-done.1 = bf16[32,2,8192]{2,1,0:T(2,128)(2,1)} async-done(((bf16[32,2,8192]{2,1,0:T(2,128)(2,1)}), bf16[32,2,8192]{2,1,0:T(2,128)(2,1)}, u32[]{:S(2)}, u32[]{:S(2)}) %all-to-all-start.1) | async-done | bytes 1048608 | tf_op jit(solution)/shard_map/all_to_all | solution.py:92
  47.8 2.3 reshape.503
  56.8 52.7 %all-gather.2.cloned.1.call-done = bf16[1024,2048]{1,0:T(8,128)(2,1)} async-done(((bf16[1024,256]{1,0:T(8,128)(2,1)}), bf16[1024,2048]{1,0:T(8,128)(2,1)}) %all-gather.2.cloned.1.call-update) | async-done | bytes 4194320 | tf_op jit(solution)/shard_map/all_gather | solution.py:104
  109.5 3.2 fusion.3
  113.0 2.6 fusion.19
  116.4 1.6 multiply_reduce_fusion
  122.5 3.3 convolution_convert_fusion.5
  126.0 116.0 %all-reduce.2.cloned.1.call-done = bf16[1024,2048]{1,0:T(8,128)(2,1)} async-done(((bf16[1024,2048]{1,0:T(8,128)(2,1)}), bf16[1024,2048]{1,0:T(8,128)(2,1)}) %all-reduce.2.cloned.1.call-update) | async-done | bytes 4194320 | tf_op jit(solution)/shard_map/psum | solution.py:157
  242.0 5.6 %fusion = (f32[1024]{0:T(1024)S(1)}, bf16[1024,2048]{1,0:T(8,128)(2,1)S(1)}) fusion(bf16[1024,2048]{1,0:T(8,128)(2,1)} %all-reduce.2.cloned.1.call-done, bf16[1024,2048]{1,0:T(8,128)(2,1)} %all-gather.2.cloned.1.call-done), kind=kLoop, calls=%fused_computation.10 | loop fusion | flops 14679040 | bytes 12587008 | tf_op jit(solution)/shard_map/reduce_sum | solution.py:21
  247.6 1.9 copy-done.2
  249.6 5.1 %fusion.13 = f32[1024,640]{1,0:T(8,128)} fusion(bf16[2048,640]{1,0:T(8,128)(2,1)S(1)} %copy-done.13, bf16[1024,2048]{1,0:T(8,128)(2,1)S(1)} %get-tuple-element.3, f32[2048]{0:T(1024)S(1)} %copy-done.17, f32[1024]{0:T(1024)S(1)} %add_rsqrt_fusion.1), kind=kOutput, calls=%fused_computation.31 | convolution fusion | flops 2692743168 | bytes 9449472 | tf_op jit(solution)/shard_map/dot_general | solution.py:162
  254.6 12.3 %convolution_convert_fusion.4 = bf16[1024,2048]{1,0:T(8,128)(2,1)} fusion(bf16[640,2048]{1,0:T(8,128)(2,1)S(1)} %copy-done, f32[1024,640]{1,0:T(8,128)} %fusion.13, bf16[2048,640]{1,0:T(8,128)(2,1)} %param.26, bf16[1024,2048]{1,0:T(8,128)(2,1)} %copy-done.2, f32[2048]{0:T(1024)S(1)} %copy-done.17, f32[1024]{0:T(1024)S(1)} %add_rsqrt_fusion.1), kind=kOutput, calls=%fused_computation.19 | convolution fusion | flops 5383127040 | bytes 16265216 | tf_op jit(solution)/shard_map/dot_general | solution.py:166
  267.0 59.3 %reduce-scatter.2.cloned.1.call-done = bf16[1024,256]{1,0:T(8,128)(2,1)} async-done(((bf16[1024,2048]{1,0:T(8,128)(2,1)}), bf16[1024,256]{1,0:T(8,128)(2,1)}) %reduce-scatter.2.cloned.1.call-update) | async-done | bytes 524304 | tf_op jit(solution)/shard_map/reduce_scatter | solution.py:165
  328.7 2.5 convolution_convert_fusion
  331.2 2.5 reshape.515
  333.7 6.5 %all-to-all-start.2 = ((bf16[32,2,8192]{2,1,0:T(2,128)(2,1)}), bf16[32,2,8192]{2,1,0:T(2,128)(2,1)}, u32[]{:S(2)}, u32[]{:S(2)}) async-start(bf16[32,2,8192]{2,1,0:T(2,128)(2,1)} %reshape.515), calls=%async_computation.3 | async-start | bytes 2097152 | tf_op jit(solution)/shard_map/all_to_all | solution.py:176
  341.2 15.5 %all-to-all-done.2 = bf16[32,2,8192]{2,1,0:T(2,128)(2,1)} async-done(((bf16[32,2,8192]{2,1,0:T(2,128)(2,1)}), bf16[32,2,8192]{2,1,0:T(2,128)(2,1)}, u32[]{:S(2)}, u32[]{:S(2)}) %all-to-all-start.2) | async-done | bytes 1048608 | tf_op jit(solution)/shard_map/all_to_all | solution.py:176
  356.6 2.3 reshape.516
  358.9 1.6 convolution_convert_fusion.2
  (95 shorter events, 21.2 us)
Async XLA Ops:
  7.2 247.5 %copy-start = (bf16[640,2048]{1,0:T(8,128)(2,1)S(1)}, bf16[640,2048]{1,0:T(8,128)(2,1)}, u32[]{:S(2)}) copy-start(bf16[640,2048]{1,0:T(8,128)(2,1)} %param.27) | copy-start | bytes 7864324
  9.8 15.4 %all-to-all-start = ((s32[32,1,2]{2,1,0:T(1,128)}), s32[32,1,2]{2,1,0:T(1,128)S(1)}, u32[]{:S(2)}, u32[]{:S(2)}) async-start(s32[32,1,2]{2,1,0:T(1,128)} %bitcast.5), calls=%async_computation | async-start | bytes 32768 | tf_op jit(solution)/shard_map/all_to_all | solution.py:95
  23.5 29.4 %copy-start.10 = (s32[1,1024]{1,0:T(1,128)S(1)}, s32[1,1024]{1,0:T(1,128)}, u32[]{:S(2)}) copy-start(s32[1,1024]{1,0:T(1,128)} %param.16) | copy-start | bytes 12292
  25.2 22.6 %all-to-all-start.1 = ((bf16[32,2,8192]{2,1,0:T(2,128)(2,1)}), bf16[32,2,8192]{2,1,0:T(2,128)(2,1)}, u32[]{:S(2)}, u32[]{:S(2)}) async-start(bf16[32,2,8192]{2,1,0:T(2,128)(2,1)} %reshape.502), calls=%async_computation.1 | async-start | bytes 2097152 | tf_op jit(solution)/shard_map/all_to_all | solution.py:92
  31.5 78.0 %all-gather.2.cloned.1.call-start = ((), (), s32[]{:S(2)}) async-start(), calls=%async_computation.4 | async-start | bytes 4718592 | tf_op jit(solution)/shard_map/all_gather | solution.py:104
  50.1 62.7 %copy-start.15 = (f32[2048]{0:T(1024)S(1)}, f32[2048]{0:T(1024)}, u32[]{:S(2)}) copy-start(f32[2048]{0:T(1024)} %param.18) | copy-start | bytes 24580
  52.6 189.4 %all-reduce.2.cloned.1.call-start = ((), (), s32[]{:S(2)}) async-start(), calls=%async_computation.5 | async-start | bytes 8388608 | tf_op jit(solution)/shard_map/psum | solution.py:157
  109.5 3.4 copy-start.1
  113.0 2.7 copy-start.11
  113.0 3.4 copy-start.14
  113.0 3.4 copy-start.16
  116.4 2.6 copy-start.6
  116.4 2.6 copy-start.8
  116.4 1.6 copy-start.12
  116.4 1.8 copy-start.5
  125.8 123.8 %copy-start.17 = (f32[2048]{0:T(1024)S(1)}, f32[2048]{0:T(1024)}, u32[]{:S(2)}) copy-start(f32[2048]{0:T(1024)} %param.24) | copy-start | bytes 24580
  125.8 200.5 %reduce-scatter.2.cloned.1.call-start = ((), (), s32[]{:S(2)}) async-start(), calls=%async_computation.6 | async-start | bytes 4718592 | tf_op jit(solution)/shard_map/reduce_scatter | solution.py:165
  242.0 7.5 %copy-start.13 = (bf16[2048,640]{1,0:T(8,128)(2,1)S(1)}, bf16[2048,640]{1,0:T(8,128)(2,1)}, u32[]{:S(2)}) copy-start(bf16[2048,640]{1,0:T(8,128)(2,1)} %param.25) | copy-start | bytes 7864324
  247.6 1.9 copy-start.2
  267.0 73.3 %copy-start.18 = (s32[1,8]{1,0:T(1,128)S(1)}, s32[1,8]{1,0:T(1,128)}, u32[]{:S(2)}) copy-start(s32[1,8]{1,0:T(1,128)} %param.17) | copy-start | bytes 100
  267.0 73.3 %copy-start.7 = (bf16[1024,1,32]{0,2,1:T(8,128)(2,1)S(1)}, bf16[1024,1,32]{0,2,1:T(8,128)(2,1)}, u32[]{:S(2)}) copy-start(bf16[1024,1,32]{0,2,1:T(8,128)(2,1)} %copy-done.6) | copy-start | bytes 196612
  267.0 73.3 %copy-start.9 = (bf16[1024,1,32]{0,2,1:T(8,128)(2,1)S(1)}, bf16[1024,1,32]{0,2,1:T(8,128)(2,1)}, u32[]{:S(2)}) copy-start(bf16[1024,1,32]{0,2,1:T(8,128)(2,1)} %copy-done.8) | copy-start | bytes 196612
  333.7 22.9 %all-to-all-start.2 = ((bf16[32,2,8192]{2,1,0:T(2,128)(2,1)}), bf16[32,2,8192]{2,1,0:T(2,128)(2,1)}, u32[]{:S(2)}, u32[]{:S(2)}) async-start(bf16[32,2,8192]{2,1,0:T(2,128)(2,1)} %reshape.515), calls=%async_computation.3 | async-start | bytes 2097152 | tf_op jit(solution)/shard_map/all_to_all | solution.py:176
  341.2 20.4 %copy-start.3 = (bf16[8,128,64]{1,2,0:T(8,128)(2,1)}, bf16[8,128,64]{1,2,0:T(8,128)(2,1)S(1)}, u32[]{:S(2)}) copy-start(bf16[8,128,64]{1,2,0:T(8,128)(2,1)S(1)} %scatter_fusion) | copy-start | bytes 393220
  (1 other events, 1.0 us)
Sparse Core Ops, SparseCore 0:
  52.8 56.6 all-gather.1
  125.9 116.0 all-reduce.1
  267.1 59.1 reduce-scatter.1
where the time goes:
time: 369 us; the launch traced here: 368 us
  waiting for transfers between devices  260 us (70%)
  matrix products  35.9 us (10%)
  starting transfers between devices  21.8 us (6%)
  local copies, waits for them, and re-layouts  19.4 us (5%)
  other arithmetic  16.1 us (4%)
  between operations  14.9 us (4%)
    psum x1, waiting for transfers between devices, on_device(): lax.psum(jnp.dot(attended, w_out, preferred_element_type=jnp.float32).ast...  116 us
    reduce_scatter x1, waiting for transfers between devices, on_device(): lax.psum_scatter(jnp.dot(hidden, w_down, preferred_element_type=jnp.float...  59.3 us
    all_gather x1, waiting for transfers between devices, on_device(): full = lax.all_gather(grouped, 'tensor', axis=1, tiled=True)  52.7 us
    all_to_all x1, waiting for transfers between devices, on_device(): lax.all_to_all(back.reshape(groups, MOST, width), 'dp', split_axis=0, con...  15.5 us
    all_to_all x1, waiting for transfers between devices, on_device(): lax.all_to_all(packed.reshape(groups, MOST, width), 'dp', split_axis=0, c...  14.9 us
    dot_general x1, matrix products, on_device(): jnp.dot(hidden, w_down, preferred_element_type=jnp.float32)  12.3 us
    reduce_sum x3, other arithmetic, rms_scale(): mean_sq = jnp.mean(values * values, axis=-1, keepdims=True)  8.85 us
    all_to_all x1, starting transfers between devices, on_device(): lax.all_to_all(slot_pos.reshape(groups, MOST), 'dp', split_axis=0, concat...  8.39 us
  transfers between devices with their start and end apart: 6, of which 6 were waited for; matrix products, arithmetic and copies ran while one was open for 3% of the time, Pallas kernels for 0%

commit v1 on v0

--- a/solution.py
+++ b/solution.py
@@ -85,22 +85,22 @@
     filled = jnp.any(send_hot, axis=1)
     slot_pos = jnp.where(filled, jnp.sum(jnp.where(send_hot, position[None, :], 0), axis=1), -1)
     send_matrix = send_hot.astype(jnp.bfloat16)
+    w_out_full = lax.all_gather(w_out, "tensor", axis=0, tiled=True)
     packed = jnp.dot(
         send_matrix, arrivals.reshape(units, width), preferred_element_type=jnp.float32
     ).astype(jnp.bfloat16)
-    received, recv_pos = (
-        lax.all_to_all(
-            packed.reshape(groups, MOST, width), "dp", split_axis=0, concat_axis=0, tiled=True
-        ),
-        lax.all_to_all(
-            slot_pos.reshape(groups, MOST), "dp", split_axis=0, concat_axis=0, tiled=True
-        ),
-    )
-    recv_matrix = (recv_pos.reshape(-1)[None, :] == unit_index[:, None]).astype(jnp.bfloat16)
+    pos_cols = jnp.broadcast_to(slot_pos.astype(jnp.bfloat16)[:, None], (slot_count, 128))
+    packed = jnp.concatenate([packed, pos_cols], axis=1)
+    received = lax.all_to_all(
+        packed.reshape(groups, MOST, width + 128), "dp", split_axis=0, concat_axis=0, tiled=True
+    ).reshape(slot_count, width + 128)
+    recv_pos = received[:, width].astype(jnp.int32)
+    recv_matrix = (recv_pos[None, :] == unit_index[:, None]).astype(jnp.bfloat16)
     grouped = jnp.dot(
-        recv_matrix, received.reshape(slot_count, width), preferred_element_type=jnp.float32
+        recv_matrix, received[:, :width], preferred_element_type=jnp.float32
     ).astype(jnp.bfloat16)
     grouped = grouped.reshape(tok_grp, feat_part)
+    grouped, w_out_full = lax.optimization_barrier((grouped, w_out_full))
     full = lax.all_gather(grouped, "tensor", axis=1, tiled=True)
     normed = rms_scale(full, attn_gain).astype(jnp.bfloat16)
     seg_row = seg_ids[0]
@@ -154,9 +154,8 @@
         )
         outputs.append(mixed.astype(jnp.bfloat16).reshape(block, q_heads * HEAD))
     attended = jnp.concatenate(outputs, axis=0)
-    attn_sum = lax.psum(
-        jnp.dot(attended, w_out, preferred_element_type=jnp.float32).astype(jnp.bfloat16), "tensor"
-    ).astype(jnp.float32)
+    attended_full = lax.all_gather(attended, "tensor", axis=1, tiled=True)
+    attn_sum = jnp.dot(attended_full, w_out_full, preferred_element_type=jnp.float32)
     middle = (full.astype(jnp.float32) + attn_sum).astype(jnp.bfloat16)
     ffn_in = rms_scale(middle, ffn_gain).astype(jnp.bfloat16)
     gate = jnp.dot(ffn_in, w_gate, preferred_element_type=jnp.float32)

time: 369 us -> 311 us (0.84)
  waiting for transfers between devices: 260 us -> 173 us
  blocking collectives: 0 us -> 44.4 us
  starting transfers between devices: 21.8 us -> 7.09 us
  matrix products: 35.9 us -> 41.1 us
  other arithmetic: 16.1 us -> 12.3 us
    psum x1 -> x0, waiting for transfers between devices: 116 us -> none  [on_device(): lax.psum(jnp.dot(attended, w_out, preferred_element_type=jnp.float32).ast...]
    all_to_all x0 -> x1, blocking collectives: none -> 44.4 us  [on_device(): lax.all_to_all(packed.reshape(groups, MOST, width + 128), 'dp', split_axi...]
    all_gather x0 -> x2, waiting for transfers between devices: none -> 43.4 us  [the longest x1 33.7 us: on_device(): attended_full = lax.all_gather(attended, 'tensor', axis=1, tiled=True)]
    all_to_all x2 -> x0, waiting for transfers between devices: 16.6 us -> none  [the longest x1 14.9 us: on_device(): lax.all_to_all(packed.reshape(groups, MOST, width), 'dp', split_axis=0, c...]
    all_to_all x2 -> x0, starting transfers between devices: 14.7 us -> none  [the longest x1 8.39 us: on_device(): lax.all_to_all(slot_pos.reshape(groups, MOST), 'dp', split_axis=0, concat...]
    dot_general x2, matrix products: 4.77 us -> 10.9 us  [the longest x1 9.41 us: on_device(): jnp.dot(attended_full, w_out_full, preferred_element_type=jnp.float32)]
    reduce_sum x3 -> x2, other arithmetic: 8.85 us -> 3.25 us  [rms_scale(): mean_sq = jnp.mean(values * values, axis=-1, keepdims=True)]
  transfers between devices with their start and end apart: 6 -> 5, of which waited for: 6 -> 5; matrix products, arithmetic and copies ran while one was open for 3% -> 5% of each run, Pallas kernels for 0% -> 0%
where the time goes in v1:
time: 311 us
  waiting for transfers between devices  173 us (56%)
  blocking collectives  44.4 us (14%)
  matrix products  41.1 us (13%)
  local copies, waits for them, and re-layouts  17.6 us (6%)
  between operations  14.9 us (5%)
  other arithmetic  12.3 us (4%)
  starting transfers between devices  7.09 us (2%)
    reduce_scatter x1, waiting for transfers between devices, on_device(): lax.psum_scatter(jnp.dot(hidden, w_down, preferred_element_type=jnp.float...  59.4 us
    all_gather x1, waiting for transfers between devices, on_device(): full = lax.all_gather(grouped, 'tensor', axis=1, tiled=True)  54.4 us
    all_to_all x1, blocking collectives, on_device(): lax.all_to_all(packed.reshape(groups, MOST, width + 128), 'dp', split_axi...  44.4 us
    all_gather x1, waiting for transfers between devices, on_device(): attended_full = lax.all_gather(attended, 'tensor', axis=1, tiled=True)  33.7 us
    all_to_all x1, waiting for transfers between devices, on_device(): lax.all_to_all(back.reshape(groups, MOST, width), 'dp', split_axis=0, con...  15.5 us
    dot_general x1, matrix products, on_device(): jnp.dot(hidden, w_down, preferred_element_type=jnp.float32)  12.3 us
    all_gather x1, waiting for transfers between devices, on_device(): w_out_full = lax.all_gather(w_out, 'tensor', axis=0, tiled=True)  9.7 us
    dot_general x1, matrix products, on_device(): jnp.dot(attended_full, w_out_full, preferred_element_type=jnp.float32)  9.41 us
  transfers between devices with their start and end apart: 5, of which 5 were waited for; matrix products, arithmetic and copies ran while one was open for 5% of the time, Pallas kernels for 0%

profile of v1, /device:TPU:65, one launch (start us, length us, event | category | flops | bytes accessed | tf_op | source)
XLA Modules:
  0.0 310.7 jit_solution(14780573403719473581)
XLA Ops:
  8.0 1.3 reshape.488
  12.7 2.3 reshape.489
  15.0 44.4 %all_to_all.10 = bf16[32,2,8320]{2,1,0:T(2,128)(2,1)} all-to-all(bf16[32,2,8320]{2,1,0:T(2,128)(2,1)} %reshape.489), channel_id=1, replica_groups=mesh['dp'=32,'tensor'=8] {'dp'}, dimensions={0} | all-to-all | bytes 2129920 | tf_op jit(solution)/shard_map/all_to_all | solution.py:94
  59.4 2.3 reshape.490
  62.5 1.5 convolution_convert_fusion.3
  65.1 9.7 %all-gather.4.cloned.1.call-done = bf16[1024,2048]{1,0:T(8,128)(2,1)} async-done(((bf16[128,2048]{1,0:T(8,128)(2,1)}), bf16[1024,2048]{1,0:T(8,128)(2,1)}) %all-gather.4.cloned.1.call-update) | async-done | bytes 4194320 | tf_op jit(solution)/shard_map/all_gather | solution.py:88
  79.0 54.4 %all-gather.6.cloned.1.call-done = bf16[1024,2048]{1,0:T(8,128)(2,1)} async-done(((bf16[1024,256]{1,0:T(8,128)(2,1)}), bf16[1024,2048]{1,0:T(8,128)(2,1)}) %all-gather.6.cloned.1.call-update) | async-done | bytes 4194320 | tf_op jit(solution)/shard_map/all_gather | solution.py:104
  133.4 3.2 %fusion.3 = f32[1024]{0:T(1024)S(1)} fusion(bf16[1024,2048]{1,0:T(8,128)(2,1)} %all-gather.6.cloned.1.call-done), kind=kLoop, calls=%fused_computation.13 | loop fusion | flops 6290432 | bytes 4198400 | tf_op jit(solution)/shard_map/reduce_sum | solution.py:21
  136.8 2.6 fusion.19
  140.3 1.6 multiply_reduce_fusion
  144.0 1.3 fusion.21
  147.1 33.7 %all-gather.8.cloned.1.call-done = bf16[1024,1024]{0,1:T(8,128)(2,1)} async-done(((bf16[1024,128]{0,1:T(8,128)(2,1)}), bf16[1024,1024]{0,1:T(8,128)(2,1)}) %all-gather.8.cloned.1.call-update) | async-done | bytes 2097168 | tf_op jit(solution)/shard_map/all_gather | solution.py:157
  180.8 9.4 %fusion = (f32[1024]{0:T(1024)S(1)}, bf16[1024,2048]{1,0:T(8,128)(2,1)S(1)}) fusion(bf16[1024,1024]{0,1:T(8,128)(2,1)} %all-gather.8.cloned.1.call-done, bf16[1024,2048]{1,0:T(8,128)(2,1)} %all-gather.4.cloned.1.call-done, bf16[1024,2048]{1,0:T(8,128)(2,1)} %all-gather.6.cloned.1.call-done), kind=kOutput, calls=%fused_computation.10 | convolution fusion | flops 4307549184 | bytes 14684160 | tf_op jit(solution)/shard_map/dot_general | solution.py:158
  190.2 1.9 copy-done.8
  192.1 5.1 %fusion.13 = f32[1024,640]{1,0:T(8,128)} fusion(bf16[2048,640]{1,0:T(8,128)(2,1)S(1)} %copy-done.12, bf16[1024,2048]{1,0:T(8,128)(2,1)S(1)} %get-tuple-element.25, f32[2048]{0:T(1024)S(1)} %copy-done.16, f32[1024]{0:T(1024)S(1)} %add_rsqrt_fusion.1), kind=kOutput, calls=%fused_computation.30 | convolution fusion | flops 2692743168 | bytes 9449472 | tf_op jit(solution)/shard_map/dot_general | solution.py:161
  197.2 12.3 %convolution_convert_fusion.4 = bf16[1024,2048]{1,0:T(8,128)(2,1)} fusion(bf16[640,2048]{1,0:T(8,128)(2,1)S(1)} %copy-done, f32[1024,640]{1,0:T(8,128)} %fusion.13, bf16[2048,640]{1,0:T(8,128)(2,1)} %param.26, bf16[1024,2048]{1,0:T(8,128)(2,1)} %copy-done.8, f32[2048]{0:T(1024)S(1)} %copy-done.16, f32[1024]{0:T(1024)S(1)} %add_rsqrt_fusion.1), kind=kOutput, calls=%fused_computation.19 | convolution fusion | flops 5383127040 | bytes 16265216 | tf_op jit(solution)/shard_map/dot_general | solution.py:165
  209.5 59.4 %reduce-scatter.2.cloned.1.call-done = bf16[1024,256]{1,0:T(8,128)(2,1)} async-done(((bf16[1024,2048]{1,0:T(8,128)(2,1)}), bf16[1024,256]{1,0:T(8,128)(2,1)}) %reduce-scatter.2.cloned.1.call-update) | async-done | bytes 524304 | tf_op jit(solution)/shard_map/reduce_scatter | solution.py:164
  268.9 1.3 add_convert_fusion
  271.3 2.5 convolution_convert_fusion
  273.8 2.5 reshape.502
  276.4 6.5 %all-to-all-start.1 = ((bf16[32,2,8192]{2,1,0:T(2,128)(2,1)}), bf16[32,2,8192]{2,1,0:T(2,128)(2,1)}, u32[]{:S(2)}, u32[]{:S(2)}) async-start(bf16[32,2,8192]{2,1,0:T(2,128)(2,1)} %reshape.502), calls=%async_computation.2 | async-start | bytes 2097152 | tf_op jit(solution)/shard_map/all_to_all | solution.py:175
  283.8 15.5 %all-to-all-done.1 = bf16[32,2,8192]{2,1,0:T(2,128)(2,1)} async-done(((bf16[32,2,8192]{2,1,0:T(2,128)(2,1)}), bf16[32,2,8192]{2,1,0:T(2,128)(2,1)}, u32[]{:S(2)}, u32[]{:S(2)}) %all-to-all-start.1) | async-done | bytes 1048608 | tf_op jit(solution)/shard_map/all_to_all | solution.py:175
  299.3 2.3 reshape.503
  301.6 1.6 convolution_convert_fusion.2
  (92 shorter events, 17.3 us)
Async XLA Ops:
  7.2 190.0 %copy-start = (bf16[640,2048]{1,0:T(8,128)(2,1)S(1)}, bf16[640,2048]{1,0:T(8,128)(2,1)}, u32[]{:S(2)}) copy-start(bf16[640,2048]{1,0:T(8,128)(2,1)} %param.27) | copy-start | bytes 7864324
  7.2 67.6 %all-gather.4.cloned.1.call-start = ((), (), s32[]{:S(2)}) async-start(), calls=%async_computation.3 | async-start | bytes 4718592 | tf_op jit(solution)/shard_map/all_gather | solution.py:88
  7.9 125.5 %all-gather.6.cloned.1.call-start = ((), (), s32[]{:S(2)}) async-start(), calls=%async_computation.4 | async-start | bytes 4718592 | tf_op jit(solution)/shard_map/all_gather | solution.py:104
  15.0 60.1 %copy-start.9 = (s32[1,1024]{1,0:T(1,128)S(1)}, s32[1,1024]{1,0:T(1,128)}, u32[]{:S(2)}) copy-start(s32[1,1024]{1,0:T(1,128)} %param.16) | copy-start | bytes 12292
  62.5 74.1 %copy-start.14 = (f32[2048]{0:T(1024)S(1)}, f32[2048]{0:T(1024)}, u32[]{:S(2)}) copy-start(f32[2048]{0:T(1024)} %param.18) | copy-start | bytes 24580
  74.8 106.0 %all-gather.8.cloned.1.call-start = ((), (), s32[]{:S(2)}) async-start(), calls=%async_computation.5 | async-start | bytes 2359296 | tf_op jit(solution)/shard_map/all_gather | solution.py:157
  133.4 3.4 %copy-start.1 = (bf16[1024,2048]{1,0:T(8,128)(2,1)S(1)}, bf16[1024,2048]{1,0:T(8,128)(2,1)}, u32[]{:S(2)}) copy-start(bf16[1024,2048]{1,0:T(8,128)(2,1)} %all-gather.6.cloned.1.call-done) | copy-start | bytes 12582916
  136.8 2.7 copy-start.10
  136.8 3.4 %copy-start.13 = (bf16[2048,128]{1,0:T(8,128)(2,1)S(1)}, bf16[2048,128]{1,0:T(8,128)(2,1)}, u32[]{:S(2)}) copy-start(bf16[2048,128]{1,0:T(8,128)(2,1)} %param.19) | copy-start | bytes 1572868
  136.8 3.4 %copy-start.15 = (f32[2048]{0:T(1024)S(1)}, f32[2048]{0:T(1024)}, u32[]{:S(2)}) copy-start(f32[2048]{0:T(1024)} %param.18) | copy-start | bytes 24580
  140.2 2.6 copy-start.4
  140.2 2.6 copy-start.6
  140.3 1.6 copy-start.11
  140.3 1.8 copy-start.3
  146.8 45.3 %copy-start.16 = (f32[2048]{0:T(1024)S(1)}, f32[2048]{0:T(1024)}, u32[]{:S(2)}) copy-start(f32[2048]{0:T(1024)} %param.24) | copy-start | bytes 24580
  146.8 122.1 %reduce-scatter.2.cloned.1.call-start = ((), (), s32[]{:S(2)}) async-start(), calls=%async_computation.6 | async-start | bytes 4718592 | tf_op jit(solution)/shard_map/reduce_scatter | solution.py:164
  180.8 11.4 %copy-start.12 = (bf16[2048,640]{1,0:T(8,128)(2,1)S(1)}, bf16[2048,640]{1,0:T(8,128)(2,1)}, u32[]{:S(2)}) copy-start(bf16[2048,640]{1,0:T(8,128)(2,1)} %param.25) | copy-start | bytes 7864324
  190.2 1.9 copy-start.8
  209.5 73.4 %copy-start.17 = (s32[1,8]{1,0:T(1,128)S(1)}, s32[1,8]{1,0:T(1,128)}, u32[]{:S(2)}) copy-start(s32[1,8]{1,0:T(1,128)} %param.17) | copy-start | bytes 100
  209.5 73.4 %copy-start.5 = (bf16[1024,1,32]{0,2,1:T(8,128)(2,1)S(1)}, bf16[1024,1,32]{0,2,1:T(8,128)(2,1)}, u32[]{:S(2)}) copy-start(bf16[1024,1,32]{0,2,1:T(8,128)(2,1)} %copy-done.4) | copy-start | bytes 196612
  209.5 73.4 %copy-start.7 = (bf16[1024,1,32]{0,2,1:T(8,128)(2,1)S(1)}, bf16[1024,1,32]{0,2,1:T(8,128)(2,1)}, u32[]{:S(2)}) copy-start(bf16[1024,1,32]{0,2,1:T(8,128)(2,1)} %copy-done.6) | copy-start | bytes 196612
  276.4 22.9 %all-to-all-start.1 = ((bf16[32,2,8192]{2,1,0:T(2,128)(2,1)}), bf16[32,2,8192]{2,1,0:T(2,128)(2,1)}, u32[]{:S(2)}, u32[]{:S(2)}) async-start(bf16[32,2,8192]{2,1,0:T(2,128)(2,1)} %reshape.502), calls=%async_computation.2 | async-start | bytes 2097152 | tf_op jit(solution)/shard_map/all_to_all | solution.py:175
  283.8 20.4 %copy-start.2 = (bf16[8,128,64]{1,2,0:T(8,128)(2,1)}, bf16[8,128,64]{1,2,0:T(8,128)(2,1)S(1)}, u32[]{:S(2)}) copy-start(bf16[8,128,64]{1,2,0:T(8,128)(2,1)S(1)} %scatter_fusion) | copy-start | bytes 393220
Sparse Core Ops, SparseCore 0:
  9.8 64.8 all-gather.3
  77.2 56.1 all-gather.5
  146.9 33.7 all-gather.7
  209.6 59.2 reduce-scatter.1

commit v2 on v1

--- a/solution.py
+++ b/solution.py
@@ -75,30 +75,33 @@
     width = unit_rows * feat_part
     dest_row = deal[0]
     target = dest_row // units
-    position = dest_row % units
     unit_index = jnp.arange(units, dtype=jnp.int32)
     earlier = unit_index[:, None] > unit_index[None, :]
     same_target = target[:, None] == target[None, :]
     rank = jnp.sum(jnp.logical_and(earlier, same_target), axis=1)
     slot = target * MOST + rank
-    send_hot = slot[None, :] == jnp.arange(slot_count, dtype=jnp.int32)[:, None]
-    filled = jnp.any(send_hot, axis=1)
-    slot_pos = jnp.where(filled, jnp.sum(jnp.where(send_hot, position[None, :], 0), axis=1), -1)
-    send_matrix = send_hot.astype(jnp.bfloat16)
+    slot_index = jnp.arange(slot_count, dtype=jnp.int32)
+    send_hot = slot[None, :] == slot_index[:, None]
+    send_src = jnp.sum(jnp.where(send_hot, unit_index[None, :], 0), axis=1)
     w_out_full = lax.all_gather(w_out, "tensor", axis=0, tiled=True)
-    packed = jnp.dot(
-        send_matrix, arrivals.reshape(units, width), preferred_element_type=jnp.float32
-    ).astype(jnp.bfloat16)
-    pos_cols = jnp.broadcast_to(slot_pos.astype(jnp.bfloat16)[:, None], (slot_count, 128))
-    packed = jnp.concatenate([packed, pos_cols], axis=1)
+    deal_all = lax.all_gather(deal, "dp", axis=0, tiled=True)
+    own_group = lax.axis_index("dp")
+    tgt_all = deal_all // units
+    same_all = tgt_all[:, :, None] == tgt_all[:, None, :]
+    rank_all = jnp.sum(jnp.logical_and(earlier[None], same_all), axis=2)
+    slot_all = jnp.arange(groups, dtype=jnp.int32)[:, None] * MOST + rank_all
+    mine = tgt_all == own_group
+    pos_all = deal_all % units
+    pos_hot = jnp.logical_and(mine[None], pos_all[None] == unit_index[:, None, None])
+    slot_of_pos = jnp.sum(jnp.where(pos_hot, slot_all[None], 0), axis=(1, 2))
+    back_hot = jnp.logical_and(mine[None], slot_all[None] == slot_index[:, None, None])
+    pos_of_slot = jnp.sum(jnp.where(back_hot, pos_all[None], 0), axis=(1, 2))
+    arrival_units = arrivals.reshape(units, unit_rows, feat_part)
+    packed = jnp.take(arrival_units, send_src, axis=0, mode="clip")
     received = lax.all_to_all(
-        packed.reshape(groups, MOST, width + 128), "dp", split_axis=0, concat_axis=0, tiled=True
-    ).reshape(slot_count, width + 128)
-    recv_pos = received[:, width].astype(jnp.int32)
-    recv_matrix = (recv_pos[None, :] == unit_index[:, None]).astype(jnp.bfloat16)
-    grouped = jnp.dot(
-        recv_matrix, received[:, :width], preferred_element_type=jnp.float32
-    ).astype(jnp.bfloat16)
+        packed.reshape(groups, MOST, unit_rows, feat_part), "dp", split_axis=0, concat_axis=0, tiled=True
+    ).reshape(slot_count, unit_rows, feat_part)
+    grouped = jnp.take(received, slot_of_pos, axis=0, mode="clip")
     grouped = grouped.reshape(tok_grp, feat_part)
     grouped, w_out_full = lax.optimization_barrier((grouped, w_out_full))
     full = lax.all_gather(grouped, "tensor", axis=1, tiled=True)
@@ -169,15 +172,11 @@
     ).astype(jnp.float32)
     own_cols = lax.dynamic_slice_in_dim(middle, tensor_rank * feat_part, feat_part, 1)
     combined = (own_cols.astype(jnp.float32) + ffn_part).astype(jnp.bfloat16)
-    back = jnp.dot(
-        recv_matrix.T, combined.reshape(units, width), preferred_element_type=jnp.float32
-    ).astype(jnp.bfloat16)
+    back = jnp.take(combined.reshape(units, unit_rows, feat_part), pos_of_slot, axis=0, mode="clip")
     returned = lax.all_to_all(
-        back.reshape(groups, MOST, width), "dp", split_axis=0, concat_axis=0, tiled=True
-    )
-    result = jnp.dot(
-        send_matrix.T, returned.reshape(slot_count, width), preferred_element_type=jnp.float32
-    ).astype(jnp.bfloat16)
+        back.reshape(groups, MOST, unit_rows, feat_part), "dp", split_axis=0, concat_axis=0, tiled=True
+    ).reshape(slot_count, unit_rows, feat_part)
+    result = jnp.take(returned, slot, axis=0, mode="clip")
     return (result.reshape(tok_grp, feat_part), kv_pages)
 
 

time: 311 us -> 364 us (1.17)
  blocking collectives: 44.4 us -> 90.5 us
  starting transfers between devices: 7.09 us -> 15.8 us
  matrix products: 41.1 us -> 34.9 us
  waiting for transfers between devices: 173 us -> 178 us
    all_gather x0 -> x1, blocking collectives: none -> 90.5 us  [on_device(): deal_all = lax.all_gather(deal, 'dp', axis=0, tiled=True)]
    all_to_all x1 -> x0, blocking collectives: 44.4 us -> none  [on_device(): lax.all_to_all(packed.reshape(groups, MOST, width + 128), 'dp', split_axi...]
    all_gather x1, waiting for transfers between devices: 54.4 us -> 70 us  [on_device(): full = lax.all_gather(grouped, 'tensor', axis=1, tiled=True)]
    reshape x8 -> x0, local copies, waits for them, and re-layouts: 13.8 us -> none  [the longest x1 2.54 us: on_device(): back.reshape(groups, MOST, width)]
    all_gather x1, waiting for transfers between devices: 9.7 us -> 0.01 us  [on_device(): w_out_full = lax.all_gather(w_out, 'tensor', axis=0, tiled=True)]
    gather x0 -> x4, local copies, waits for them, and re-layouts: none -> 9.5 us  [the longest x1 2.66 us: on_device(): packed = jnp.take(arrival_units, send_src, axis=0, mode='clip')]
    all_to_all x1 -> x2, starting transfers between devices: 6.53 us -> 15.3 us  [the longest x1 8.65 us: on_device(): lax.all_to_all(packed.reshape(groups, MOST, unit_rows, feat_part), 'dp',...]
    dot_general x4 -> x0, matrix products: 6.16 us -> none  [the longest x1 2.51 us: on_device(): jnp.dot(recv_matrix.T, combined.reshape(units, width), preferred_element_...]
  transfers between devices with their start and end apart: 5 -> 6, of which waited for: 5 -> 4; matrix products, arithmetic and copies ran while one was open for 5% -> 4% of each run, Pallas kernels for 0% -> 0%
where the time goes in v2:
time: 364 us; the launch traced here: 363 us
  waiting for transfers between devices  178 us (49%)
  blocking collectives  90.5 us (25%)
  matrix products  34.9 us (10%)
  starting transfers between devices  15.8 us (4%)
  local copies, waits for them, and re-layouts  15.1 us (4%)
  between operations  15 us (4%)
  other arithmetic  13.8 us (4%)
    all_gather x1, blocking collectives, on_device(): deal_all = lax.all_gather(deal, 'dp', axis=0, tiled=True)  90.5 us
    all_gather x1, waiting for transfers between devices, on_device(): full = lax.all_gather(grouped, 'tensor', axis=1, tiled=True)  70 us
    reduce_scatter x1, waiting for transfers between devices, on_device(): lax.psum_scatter(jnp.dot(hidden, w_down, preferred_element_type=jnp.float...  58.1 us
    all_gather x1, waiting for transfers between devices, on_device(): attended_full = lax.all_gather(attended, 'tensor', axis=1, tiled=True)  33.7 us
    all_to_all x1, waiting for transfers between devices, on_device(): lax.all_to_all(back.reshape(groups, MOST, unit_rows, feat_part), 'dp', sp...  15.4 us
    dot_general x1, matrix products, on_device(): jnp.dot(hidden, w_down, preferred_element_type=jnp.float32)  12.3 us
    dot_general x1, matrix products, on_device(): jnp.dot(attended_full, w_out_full, preferred_element_type=jnp.float32)  9.41 us
    all_to_all x1, starting transfers between devices, on_device(): lax.all_to_all(packed.reshape(groups, MOST, unit_rows, feat_part), 'dp',...  8.65 us
  transfers between devices with their start and end apart: 6, of which 4 were waited for; matrix products, arithmetic and copies ran while one was open for 4% of the time, Pallas kernels for 0%

profile of v2, /device:TPU:65, one launch (start us, length us, event | category | flops | bytes accessed | tf_op | source)
XLA Modules:
  0.0 363.1 jit_solution(4021554525653756425)
XLA Ops:
  10.3 2.7 gather_fusion
  12.9 8.7 %all-to-all-start = ((bf16[32,2,32,256]{3,2,1,0:T(8,128)(2,1)}), bf16[32,2,32,256]{3,2,1,0:T(8,128)(2,1)}, u32[]{:S(2)}, u32[]{:S(2)}) async-start(bf16[32,2,32,256]{3,2,1,0:T(8,128)(2,1)} %bitcast.156), calls=%async_computation | async-start | bytes 2097152 | tf_op jit(solution)/shard_map/all_to_all | solution.py:101
  21.7 90.5 %all-gather = s32[32,1,32]{2,1,0:T(1,128)S(1)} all-gather(s32[1,1,32]{2,1,0:T(1,128)S(1)} %bitcast.175), channel_id=1, replica_groups=mesh['dp'=32,'tensor'=8] {'dp'}, dimensions={0}, use_global_device_ids=true | all-gather | bytes 4224 | tf_op jit(solution)/shard_map/all_gather | solution.py:87
  112.2 0.8 convert_reduce_fusion
  114.4 2.6 gather_fusion.1
  120.3 1.0 compare_and_fusion
  121.8 70.0 %all-gather.7.cloned.1.call-done = bf16[1024,2048]{1,0:T(8,128)(2,1)} async-done(((bf16[1024,256]{1,0:T(8,128)(2,1)}), bf16[1024,2048]{1,0:T(8,128)(2,1)}) %all-gather.7.cloned.1.call-update) | async-done | bytes 4194320 | tf_op jit(solution)/shard_map/all_gather | solution.py:107
  191.9 3.2 fusion.3
  195.3 2.6 fusion.19
  198.1 1.2 fusion.33
  199.4 1.6 multiply_reduce_fusion
  201.9 1.1 fusion.7
  203.1 1.3 fusion.21
  206.2 33.7 %all-gather.9.cloned.1.call-done = bf16[1024,1024]{0,1:T(8,128)(2,1)} async-done(((bf16[1024,128]{0,1:T(8,128)(2,1)}), bf16[1024,1024]{0,1:T(8,128)(2,1)}) %all-gather.9.cloned.1.call-update) | async-done | bytes 2097168 | tf_op jit(solution)/shard_map/all_gather | solution.py:160
  239.8 9.4 %fusion = (f32[1024]{0:T(1024)S(1)}, bf16[1024,2048]{1,0:T(8,128)(2,1)S(1)}) fusion(bf16[1024,1024]{0,1:T(8,128)(2,1)} %all-gather.9.cloned.1.call-done, bf16[1024,2048]{1,0:T(8,128)(2,1)} %all-gather.5.cloned.1.call-done, bf16[1024,2048]{1,0:T(8,128)(2,1)} %all-gather.7.cloned.1.call-done), kind=kOutput, calls=%fused_computation.10 | convolution fusion | flops 4307549184 | bytes 14684160 | tf_op jit(solution)/shard_map/dot_general | solution.py:161
  249.3 1.9 copy-done.10
  251.2 5.1 %fusion.13 = f32[1024,640]{1,0:T(8,128)} fusion(bf16[2048,640]{1,0:T(8,128)(2,1)S(1)} %copy-done.21, bf16[1024,2048]{1,0:T(8,128)(2,1)S(1)} %get-tuple-element.25, f32[2048]{0:T(1024)S(1)} %copy-done.25, f32[1024]{0:T(1024)S(1)} %add_rsqrt_fusion.1), kind=kOutput, calls=%fused_computation.30 | convolution fusion | flops 2692743168 | bytes 9449472 | tf_op jit(solution)/shard_map/dot_general | solution.py:164
  256.3 12.3 %convolution_convert_fusion = bf16[1024,2048]{1,0:T(8,128)(2,1)} fusion(bf16[640,2048]{1,0:T(8,128)(2,1)S(1)} %copy-done, f32[1024,640]{1,0:T(8,128)} %fusion.13, bf16[2048,640]{1,0:T(8,128)(2,1)} %param.26, bf16[1024,2048]{1,0:T(8,128)(2,1)} %copy-done.10, f32[2048]{0:T(1024)S(1)} %copy-done.25, f32[1024]{0:T(1024)S(1)} %add_rsqrt_fusion.1), kind=kOutput, calls=%fused_computation.19 | convolution fusion | flops 5383127040 | bytes 16265216 | tf_op jit(solution)/shard_map/dot_general | solution.py:168
  269.9 58.1 %reduce-scatter.2.cloned.1.call-done = bf16[1024,256]{1,0:T(8,128)(2,1)} async-done(((bf16[1024,2048]{1,0:T(8,128)(2,1)}), bf16[1024,256]{1,0:T(8,128)(2,1)}) %reduce-scatter.2.cloned.1.call-update) | async-done | bytes 524304 | tf_op jit(solution)/shard_map/reduce_scatter | solution.py:167
  328.0 1.3 add_convert_fusion
  329.3 1.6 gather_fusion.2
  331.0 6.6 %all-to-all-start.1 = ((bf16[32,2,32,256]{3,2,1,0:T(8,128)(2,1)}), bf16[32,2,32,256]{3,2,1,0:T(8,128)(2,1)}, u32[]{:S(2)}, u32[]{:S(2)}) async-start(bf16[32,2,32,256]{3,2,1,0:T(8,128)(2,1)} %bitcast.155), calls=%async_computation.2 | async-start | bytes 2097152 | tf_op jit(solution)/shard_map/all_to_all | solution.py:176
  338.6 15.4 %all-to-all-done.1 = bf16[32,2,32,256]{3,2,1,0:T(8,128)(2,1)} async-done(((bf16[32,2,32,256]{3,2,1,0:T(8,128)(2,1)}), bf16[32,2,32,256]{3,2,1,0:T(8,128)(2,1)}, u32[]{:S(2)}, u32[]{:S(2)}) %all-to-all-start.1) | async-done | bytes 1048608 | tf_op jit(solution)/shard_map/all_to_all | solution.py:176
  354.0 2.6 gather_fusion.3
  (115 shorter events, 12.8 us)
Async XLA Ops:
  7.2 249.1 %copy-start = (bf16[640,2048]{1,0:T(8,128)(2,1)S(1)}, bf16[640,2048]{1,0:T(8,128)(2,1)}, u32[]{:S(2)}) copy-start(bf16[640,2048]{1,0:T(8,128)(2,1)} %param.27) | copy-start | bytes 7864324
  7.2 14.5 %copy-start.19 = (s32[1,32]{1,0:T(1,128)S(1)}, s32[1,32]{1,0:T(1,128)}, u32[]{:S(2)}) copy-start(s32[1,32]{1,0:T(1,128)} %param.15) | copy-start | bytes 388
  7.2 110.1 %copy-start.15 = (s32[1,1024]{1,0:T(1,128)S(1)}, s32[1,1024]{1,0:T(1,128)}, u32[]{:S(2)}) copy-start(s32[1,1024]{1,0:T(1,128)} %param.16) | copy-start | bytes 12292
  7.2 109.8 %all-gather.5.cloned.1.call-start = ((), (), s32[]{:S(2)}) async-start(), calls=%async_computation.3 | async-start | bytes 4718592 | tf_op jit(solution)/shard_map/all_gather | solution.py:86
  12.9 182.1 %copy-start.23 = (f32[2048]{0:T(1024)S(1)}, f32[2048]{0:T(1024)}, u32[]{:S(2)}) copy-start(f32[2048]{0:T(1024)} %param.18) | copy-start | bytes 24580
  12.9 101.4 %all-to-all-start = ((bf16[32,2,32,256]{3,2,1,0:T(8,128)(2,1)}), bf16[32,2,32,256]{3,2,1,0:T(8,128)(2,1)}, u32[]{:S(2)}, u32[]{:S(2)}) async-start(bf16[32,2,32,256]{3,2,1,0:T(8,128)(2,1)} %bitcast.156), calls=%async_computation | async-start | bytes 2097152 | tf_op jit(solution)/shard_map/all_to_all | solution.py:101
  21.6 170.2 %all-gather.7.cloned.1.call-start = ((), (), s32[]{:S(2)}) async-start(), calls=%async_computation.4 | async-start | bytes 4718592 | tf_op jit(solution)/shard_map/all_gather | solution.py:107
  117.0 122.8 %all-gather.9.cloned.1.call-start = ((), (), s32[]{:S(2)}) async-start(), calls=%async_computation.5 | async-start | bytes 2359296 | tf_op jit(solution)/shard_map/all_gather | solution.py:160
  119.0 79.0 %copy-start.16 = (f32[32]{0:T(128)}, f32[32]{0:T(128)S(1)}, u32[]{:S(2)}) copy-start(f32[32]{0:T(128)S(1)} %multiply_power_fusion) | copy-start | bytes 388
  191.8 3.4 copy-start.1
  195.3 2.7 copy-start.17
  195.3 2.8 copy-start.12
  195.3 4.0 %copy-start.22 = (bf16[2048,128]{1,0:T(8,128)(2,1)S(1)}, bf16[2048,128]{1,0:T(8,128)(2,1)}, u32[]{:S(2)}) copy-start(bf16[2048,128]{1,0:T(8,128)(2,1)} %param.19) | copy-start | bytes 1572868
  195.3 4.0 %copy-start.24 = (f32[2048]{0:T(1024)S(1)}, f32[2048]{0:T(1024)}, u32[]{:S(2)}) copy-start(f32[2048]{0:T(1024)} %param.18) | copy-start | bytes 24580
  205.9 45.3 %copy-start.25 = (f32[2048]{0:T(1024)S(1)}, f32[2048]{0:T(1024)}, u32[]{:S(2)}) copy-start(f32[2048]{0:T(1024)} %param.24) | copy-start | bytes 24580
  205.9 122.1 %reduce-scatter.2.cloned.1.call-start = ((), (), s32[]{:S(2)}) async-start(), calls=%async_computation.6 | async-start | bytes 4718592 | tf_op jit(solution)/shard_map/reduce_scatter | solution.py:167
  239.8 11.4 %copy-start.21 = (bf16[2048,640]{1,0:T(8,128)(2,1)S(1)}, bf16[2048,640]{1,0:T(8,128)(2,1)}, u32[]{:S(2)}) copy-start(bf16[2048,640]{1,0:T(8,128)(2,1)} %param.25) | copy-start | bytes 7864324
  268.6 69.1 %copy-start.20 = (s32[1,32]{1,0:T(1,128)S(1)}, s32[1,32]{1,0:T(1,128)}, u32[]{:S(2)}) copy-start(s32[1,32]{1,0:T(1,128)} %param.15) | copy-start | bytes 388
  268.6 69.1 %copy-start.28 = (s32[32]{0:T(128)S(1)}, s32[32]{0:T(128)}, u32[]{:S(2)}) copy-start(s32[32]{0:T(128)} %copy-done.27) | copy-start | bytes 388
  268.6 69.1 %copy-start.26 = (s32[1,8]{1,0:T(1,128)S(1)}, s32[1,8]{1,0:T(1,128)}, u32[]{:S(2)}) copy-start(s32[1,8]{1,0:T(1,128)} %param.17) | copy-start | bytes 100
  268.6 69.1 %copy-start.5 = (bf16[1024,1,32]{0,2,1:T(8,128)(2,1)S(1)}, bf16[1024,1,32]{0,2,1:T(8,128)(2,1)}, u32[]{:S(2)}) copy-start(bf16[1024,1,32]{0,2,1:T(8,128)(2,1)} %copy-done.4) | copy-start | bytes 196612
  268.6 69.1 %copy-start.7 = (bf16[1024,1,32]{0,2,1:T(8,128)(2,1)S(1)}, bf16[1024,1,32]{0,2,1:T(8,128)(2,1)}, u32[]{:S(2)}) copy-start(bf16[1024,1,32]{0,2,1:T(8,128)(2,1)} %copy-done.6) | copy-start | bytes 196612
  331.0 23.0 %all-to-all-start.1 = ((bf16[32,2,32,256]{3,2,1,0:T(8,128)(2,1)}), bf16[32,2,32,256]{3,2,1,0:T(8,128)(2,1)}, u32[]{:S(2)}, u32[]{:S(2)}) async-start(bf16[32,2,32,256]{3,2,1,0:T(8,128)(2,1)} %bitcast.155), calls=%async_computation.2 | async-start | bytes 2097152 | tf_op jit(solution)/shard_map/all_to_all | solution.py:176
  338.6 18.0 %copy-start.2 = (bf16[8,128,64]{1,2,0:T(8,128)(2,1)}, bf16[8,128,64]{1,2,0:T(8,128)(2,1)S(1)}, u32[]{:S(2)}) copy-start(bf16[8,128,64]{1,2,0:T(8,128)(2,1)S(1)} %scatter_fusion) | copy-start | bytes 393220
  (11 other events, 16.0 us)
Sparse Core Ops, SparseCore 0:
  9.9 63.1 all-gather.4
  117.1 74.6 all-gather.6
  206.0 33.7 all-gather.8
  268.8 59.1 reduce-scatter.1

commit v3 on v2

--- a/solution.py
+++ b/solution.py
@@ -84,24 +84,23 @@
     send_hot = slot[None, :] == slot_index[:, None]
     send_src = jnp.sum(jnp.where(send_hot, unit_index[None, :], 0), axis=1)
     w_out_full = lax.all_gather(w_out, "tensor", axis=0, tiled=True)
-    deal_all = lax.all_gather(deal, "dp", axis=0, tiled=True)
-    own_group = lax.axis_index("dp")
-    tgt_all = deal_all // units
-    same_all = tgt_all[:, :, None] == tgt_all[:, None, :]
-    rank_all = jnp.sum(jnp.logical_and(earlier[None], same_all), axis=2)
-    slot_all = jnp.arange(groups, dtype=jnp.int32)[:, None] * MOST + rank_all
-    mine = tgt_all == own_group
-    pos_all = deal_all % units
-    pos_hot = jnp.logical_and(mine[None], pos_all[None] == unit_index[:, None, None])
-    slot_of_pos = jnp.sum(jnp.where(pos_hot, slot_all[None], 0), axis=(1, 2))
-    back_hot = jnp.logical_and(mine[None], slot_all[None] == slot_index[:, None, None])
-    pos_of_slot = jnp.sum(jnp.where(back_hot, pos_all[None], 0), axis=(1, 2))
+    position = dest_row % units
+    filled = jnp.any(send_hot, axis=1)
+    slot_pos = jnp.where(filled, jnp.sum(jnp.where(send_hot, position[None, :], 0), axis=1), -1)
+    pos_block = jnp.zeros((groups, 8, feat_part), jnp.bfloat16)
+    pos_block = pos_block.at[:, 0, :MOST].set(slot_pos.reshape(groups, MOST).astype(jnp.bfloat16))
     arrival_units = arrivals.reshape(units, unit_rows, feat_part)
     packed = jnp.take(arrival_units, send_src, axis=0, mode="clip")
-    received = lax.all_to_all(
-        packed.reshape(groups, MOST, unit_rows, feat_part), "dp", split_axis=0, concat_axis=0, tiled=True
-    ).reshape(slot_count, unit_rows, feat_part)
-    grouped = jnp.take(received, slot_of_pos, axis=0, mode="clip")
+    payload = jnp.concatenate(
+        [packed.reshape(groups, MOST * unit_rows, feat_part), pos_block], axis=1
+    )
+    received = lax.all_to_all(payload, "dp", split_axis=0, concat_axis=0, tiled=True)
+    recv_pos = received[:, MOST * unit_rows, :MOST].reshape(slot_count).astype(jnp.int32)
+    recv_units = received[:, : MOST * unit_rows].reshape(slot_count, unit_rows, feat_part)
+    pos_hot = recv_pos[None, :] == unit_index[:, None]
+    slot_of_pos = jnp.sum(jnp.where(pos_hot, slot_index[None, :], 0), axis=1)
+    pos_of_slot = jnp.maximum(recv_pos, 0)
+    grouped = jnp.take(recv_units, slot_of_pos, axis=0, mode="clip")
     grouped = grouped.reshape(tok_grp, feat_part)
     grouped, w_out_full = lax.optimization_barrier((grouped, w_out_full))
     full = lax.all_gather(grouped, "tensor", axis=1, tiled=True)

time: 364 us -> 305 us (0.84)
  blocking collectives: 90.5 us -> 45.8 us
  starting transfers between devices: 15.8 us -> 6.86 us
  waiting for transfers between devices: 178 us -> 172 us
    all_gather x1 -> x0, blocking collectives: 90.5 us -> none  [on_device(): deal_all = lax.all_gather(deal, 'dp', axis=0, tiled=True)]
    all_to_all x0 -> x1, blocking collectives: none -> 45.8 us  [on_device(): lax.all_to_all(payload, 'dp', split_axis=0, concat_axis=0, tiled=True)]
    all_gather x1, waiting for transfers between devices: 70 us -> 53.1 us  [on_device(): full = lax.all_gather(grouped, 'tensor', axis=1, tiled=True)]
    all_gather x1, waiting for transfers between devices: 0.01 us -> 9.5 us  [on_device(): w_out_full = lax.all_gather(w_out, 'tensor', axis=0, tiled=True)]
    all_to_all x1 -> x0, starting transfers between devices: 8.65 us -> none  [on_device(): lax.all_to_all(packed.reshape(groups, MOST, unit_rows, feat_part), 'dp',...]
  transfers between devices with their start and end apart: 6 -> 5, of which waited for: 4 -> 5; matrix products, arithmetic and copies ran while one was open for 4% -> 5% of each run, Pallas kernels for 0% -> 0%
where the time goes in v3:
time: 305 us
  waiting for transfers between devices  172 us (56%)
  blocking collectives  45.8 us (15%)
  matrix products  34.9 us (11%)
  local copies, waits for them, and re-layouts  17.9 us (6%)
  between operations  14.9 us (5%)
  other arithmetic  12.6 us (4%)
  starting transfers between devices  6.86 us (2%)
    reduce_scatter x1, waiting for transfers between devices, on_device(): lax.psum_scatter(jnp.dot(hidden, w_down, preferred_element_type=jnp.float...  59.3 us
    all_gather x1, waiting for transfers between devices, on_device(): full = lax.all_gather(grouped, 'tensor', axis=1, tiled=True)  53.1 us
    all_to_all x1, blocking collectives, on_device(): lax.all_to_all(payload, 'dp', split_axis=0, concat_axis=0, tiled=True)  45.8 us
    all_gather x1, waiting for transfers between devices, on_device(): attended_full = lax.all_gather(attended, 'tensor', axis=1, tiled=True)  33.7 us
    all_to_all x1, waiting for transfers between devices, on_device(): lax.all_to_all(back.reshape(groups, MOST, unit_rows, feat_part), 'dp', sp...  15.4 us
    dot_general x1, matrix products, on_device(): jnp.dot(hidden, w_down, preferred_element_type=jnp.float32)  12.3 us
    all_gather x1, waiting for transfers between devices, on_device(): w_out_full = lax.all_gather(w_out, 'tensor', axis=0, tiled=True)  9.5 us
    dot_general x1, matrix products, on_device(): jnp.dot(attended_full, w_out_full, preferred_element_type=jnp.float32)  9.41 us
  transfers between devices with their start and end apart: 5, of which 5 were waited for; matrix products, arithmetic and copies ran while one was open for 5% of the time, Pallas kernels for 0%

profile of v3, /device:TPU:65, one launch (start us, length us, event | category | flops | bytes accessed | tf_op | source)
XLA Modules:
  0.0 304.8 jit_solution(16552042353088243745)
XLA Ops:
  10.2 2.6 gather_fusion
  12.9 1.3 fusion.22
  14.2 45.8 %all_to_all.10 = bf16[32,72,256]{2,1,0:T(8,128)(2,1)S(1)} all-to-all(bf16[32,72,256]{2,1,0:T(8,128)(2,1)S(1)} %fusion.22), channel_id=1, replica_groups=mesh['dp'=32,'tensor'=8] {'dp'}, dimensions={0} | all-to-all | bytes 2359296 | tf_op jit(solution)/shard_map/all_to_all | solution.py:97
  61.2 2.4 slice.126
  63.7 2.6 gather_fusion.1
  66.3 9.5 %all-gather.4.cloned.1.call-done = bf16[1024,2048]{1,0:T(8,128)(2,1)} async-done(((bf16[128,2048]{1,0:T(8,128)(2,1)}), bf16[1024,2048]{1,0:T(8,128)(2,1)}) %all-gather.4.cloned.1.call-update) | async-done | bytes 4194320 | tf_op jit(solution)/shard_map/all_gather | solution.py:86
  80.4 53.1 %all-gather.6.cloned.1.call-done = bf16[1024,2048]{1,0:T(8,128)(2,1)} async-done(((bf16[1024,256]{1,0:T(8,128)(2,1)}), bf16[1024,2048]{1,0:T(8,128)(2,1)}) %all-gather.6.cloned.1.call-update) | async-done | bytes 4194320 | tf_op jit(solution)/shard_map/all_gather | solution.py:106
  133.5 3.2 %fusion.3 = f32[1024]{0:T(1024)S(1)} fusion(bf16[1024,2048]{1,0:T(8,128)(2,1)} %all-gather.6.cloned.1.call-done), kind=kLoop, calls=%fused_computation.13 | loop fusion | flops 6290432 | bytes 4198400 | tf_op jit(solution)/shard_map/reduce_sum | solution.py:21
  137.0 2.6 fusion.20
  139.8 1.2 fusion.33
  141.1 1.6 multiply_reduce_fusion
  143.6 1.1 fusion.7
  144.8 1.3 fusion.23
  147.8 33.7 %all-gather.8.cloned.1.call-done = bf16[1024,1024]{0,1:T(8,128)(2,1)} async-done(((bf16[1024,128]{0,1:T(8,128)(2,1)}), bf16[1024,1024]{0,1:T(8,128)(2,1)}) %all-gather.8.cloned.1.call-update) | async-done | bytes 2097168 | tf_op jit(solution)/shard_map/all_gather | solution.py:159
  181.5 9.4 %fusion = (f32[1024]{0:T(1024)S(1)}, bf16[1024,2048]{1,0:T(8,128)(2,1)S(1)}) fusion(bf16[1024,1024]{0,1:T(8,128)(2,1)} %all-gather.8.cloned.1.call-done, bf16[1024,2048]{1,0:T(8,128)(2,1)} %all-gather.4.cloned.1.call-done, bf16[1024,2048]{1,0:T(8,128)(2,1)} %all-gather.6.cloned.1.call-done), kind=kOutput, calls=%fused_computation.10 | convolution fusion | flops 4307549184 | bytes 14684160 | tf_op jit(solution)/shard_map/dot_general | solution.py:160
  191.0 1.9 copy-done.9
  192.9 5.1 %fusion.14 = f32[1024,640]{1,0:T(8,128)} fusion(bf16[2048,640]{1,0:T(8,128)(2,1)S(1)} %copy-done.16, bf16[1024,2048]{1,0:T(8,128)(2,1)S(1)} %get-tuple-element.41, f32[2048]{0:T(1024)S(1)} %copy-done.20, f32[1024]{0:T(1024)S(1)} %add_rsqrt_fusion.1), kind=kOutput, calls=%fused_computation.32 | convolution fusion | flops 2692743168 | bytes 9449472 | tf_op jit(solution)/shard_map/dot_general | solution.py:163
  198.0 12.3 %convolution_convert_fusion = bf16[1024,2048]{1,0:T(8,128)(2,1)} fusion(bf16[640,2048]{1,0:T(8,128)(2,1)S(1)} %copy-done, f32[1024,640]{1,0:T(8,128)} %fusion.14, bf16[2048,640]{1,0:T(8,128)(2,1)} %param.28, bf16[1024,2048]{1,0:T(8,128)(2,1)} %copy-done.9, f32[2048]{0:T(1024)S(1)} %copy-done.20, f32[1024]{0:T(1024)S(1)} %add_rsqrt_fusion.1), kind=kOutput, calls=%fused_computation.19 | convolution fusion | flops 5383127040 | bytes 16265216 | tf_op jit(solution)/shard_map/dot_general | solution.py:167
  210.4 59.3 %reduce-scatter.2.cloned.1.call-done = bf16[1024,256]{1,0:T(8,128)(2,1)} async-done(((bf16[1024,2048]{1,0:T(8,128)(2,1)}), bf16[1024,256]{1,0:T(8,128)(2,1)}) %reduce-scatter.2.cloned.1.call-update) | async-done | bytes 524304 | tf_op jit(solution)/shard_map/reduce_scatter | solution.py:166
  269.8 1.3 add_convert_fusion
  271.1 1.6 gather_fusion.2
  272.7 6.5 %all-to-all-start.1 = ((bf16[32,2,32,256]{3,2,1,0:T(8,128)(2,1)}), bf16[32,2,32,256]{3,2,1,0:T(8,128)(2,1)}, u32[]{:S(2)}, u32[]{:S(2)}) async-start(bf16[32,2,32,256]{3,2,1,0:T(8,128)(2,1)} %bitcast.154), calls=%async_computation.2 | async-start | bytes 2097152 | tf_op jit(solution)/shard_map/all_to_all | solution.py:175
  280.2 15.4 %all-to-all-done.1 = bf16[32,2,32,256]{3,2,1,0:T(8,128)(2,1)} async-done(((bf16[32,2,32,256]{3,2,1,0:T(8,128)(2,1)}), bf16[32,2,32,256]{3,2,1,0:T(8,128)(2,1)}, u32[]{:S(2)}, u32[]{:S(2)}) %all-to-all-start.1) | async-done | bytes 1048608 | tf_op jit(solution)/shard_map/all_to_all | solution.py:175
  295.7 2.6 gather_fusion.3
  (107 shorter events, 12.3 us)
Async XLA Ops:
  7.2 190.8 %copy-start = (bf16[640,2048]{1,0:T(8,128)(2,1)S(1)}, bf16[640,2048]{1,0:T(8,128)(2,1)}, u32[]{:S(2)}) copy-start(bf16[640,2048]{1,0:T(8,128)(2,1)} %param.29) | copy-start | bytes 7864324
  7.2 68.6 %all-gather.4.cloned.1.call-start = ((), (), s32[]{:S(2)}) async-start(), calls=%async_computation.3 | async-start | bytes 4718592 | tf_op jit(solution)/shard_map/all_gather | solution.py:86
  7.9 125.6 %all-gather.6.cloned.1.call-start = ((), (), s32[]{:S(2)}) async-start(), calls=%async_computation.4 | async-start | bytes 4718592 | tf_op jit(solution)/shard_map/all_gather | solution.py:106
  12.9 63.0 %copy-start.12 = (s32[1,1024]{1,0:T(1,128)S(1)}, s32[1,1024]{1,0:T(1,128)}, u32[]{:S(2)}) copy-start(s32[1,1024]{1,0:T(1,128)} %param.18) | copy-start | bytes 12292
  61.2 75.6 %copy-start.18 = (f32[2048]{0:T(1024)S(1)}, f32[2048]{0:T(1024)}, u32[]{:S(2)}) copy-start(f32[2048]{0:T(1024)} %param.20) | copy-start | bytes 24580
  75.8 105.7 %all-gather.8.cloned.1.call-start = ((), (), s32[]{:S(2)}) async-start(), calls=%async_computation.5 | async-start | bytes 2359296 | tf_op jit(solution)/shard_map/all_gather | solution.py:159
  77.6 62.1 %copy-start.13 = (f32[32]{0:T(128)}, f32[32]{0:T(128)S(1)}, u32[]{:S(2)}) copy-start(f32[32]{0:T(128)S(1)} %multiply_power_fusion) | copy-start | bytes 388
  133.5 3.4 %copy-start.2 = (bf16[1024,2048]{1,0:T(8,128)(2,1)S(1)}, bf16[1024,2048]{1,0:T(8,128)(2,1)}, u32[]{:S(2)}) copy-start(bf16[1024,2048]{1,0:T(8,128)(2,1)} %all-gather.6.cloned.1.call-done) | copy-start | bytes 12582916
  137.0 2.7 copy-start.14
  137.0 2.8 copy-start.11
  137.0 4.0 %copy-start.17 = (bf16[2048,128]{1,0:T(8,128)(2,1)S(1)}, bf16[2048,128]{1,0:T(8,128)(2,1)}, u32[]{:S(2)}) copy-start(bf16[2048,128]{1,0:T(8,128)(2,1)} %param.21) | copy-start | bytes 1572868
  137.0 4.0 %copy-start.19 = (f32[2048]{0:T(1024)S(1)}, f32[2048]{0:T(1024)}, u32[]{:S(2)}) copy-start(f32[2048]{0:T(1024)} %param.20) | copy-start | bytes 24580
  141.0 2.6 copy-start.5
  141.0 2.6 copy-start.7
  147.6 45.3 %copy-start.20 = (f32[2048]{0:T(1024)S(1)}, f32[2048]{0:T(1024)}, u32[]{:S(2)}) copy-start(f32[2048]{0:T(1024)} %param.26) | copy-start | bytes 24580
  147.6 122.1 %reduce-scatter.2.cloned.1.call-start = ((), (), s32[]{:S(2)}) async-start(), calls=%async_computation.6 | async-start | bytes 4718592 | tf_op jit(solution)/shard_map/reduce_scatter | solution.py:166
  181.5 11.4 %copy-start.16 = (bf16[2048,640]{1,0:T(8,128)(2,1)S(1)}, bf16[2048,640]{1,0:T(8,128)(2,1)}, u32[]{:S(2)}) copy-start(bf16[2048,640]{1,0:T(8,128)(2,1)} %param.27) | copy-start | bytes 7864324
  210.3 69.0 %copy-start.21 = (s32[1,32]{1,0:T(1,128)S(1)}, s32[1,32]{1,0:T(1,128)}, u32[]{:S(2)}) copy-start(s32[1,32]{1,0:T(1,128)} %param.17) | copy-start | bytes 388
  210.3 69.0 %copy-start.24 = (s32[32]{0:T(128)S(1)}, s32[32]{0:T(128)}, u32[]{:S(2)}) copy-start(s32[32]{0:T(128)} %copy-done.23) | copy-start | bytes 388
  210.3 69.1 %copy-start.22 = (s32[1,8]{1,0:T(1,128)S(1)}, s32[1,8]{1,0:T(1,128)}, u32[]{:S(2)}) copy-start(s32[1,8]{1,0:T(1,128)} %param.19) | copy-start | bytes 100
  210.3 69.1 %copy-start.6 = (bf16[1024,1,32]{0,2,1:T(8,128)(2,1)S(1)}, bf16[1024,1,32]{0,2,1:T(8,128)(2,1)}, u32[]{:S(2)}) copy-start(bf16[1024,1,32]{0,2,1:T(8,128)(2,1)} %copy-done.5) | copy-start | bytes 196612
  210.3 69.1 %copy-start.8 = (bf16[1024,1,32]{0,2,1:T(8,128)(2,1)S(1)}, bf16[1024,1,32]{0,2,1:T(8,128)(2,1)}, u32[]{:S(2)}) copy-start(bf16[1024,1,32]{0,2,1:T(8,128)(2,1)} %copy-done.7) | copy-start | bytes 196612
  272.7 22.9 %all-to-all-start.1 = ((bf16[32,2,32,256]{3,2,1,0:T(8,128)(2,1)}), bf16[32,2,32,256]{3,2,1,0:T(8,128)(2,1)}, u32[]{:S(2)}, u32[]{:S(2)}) async-start(bf16[32,2,32,256]{3,2,1,0:T(8,128)(2,1)} %bitcast.154), calls=%async_computation.2 | async-start | bytes 2097152 | tf_op jit(solution)/shard_map/all_to_all | solution.py:175
  280.2 18.1 %copy-start.3 = (bf16[8,128,64]{1,2,0:T(8,128)(2,1)}, bf16[8,128,64]{1,2,0:T(8,128)(2,1)S(1)}, u32[]{:S(2)}) copy-start(bf16[8,128,64]{1,2,0:T(8,128)(2,1)S(1)} %scatter_fusion) | copy-start | bytes 393220
  (6 other events, 7.5 us)
Sparse Core Ops, SparseCore 0:
  9.8 65.8 all-gather.3
  78.2 55.3 all-gather.5
  147.7 33.7 all-gather.7
  210.4 59.2 reduce-scatter.1

commit v4 on v3

--- a/solution.py
+++ b/solution.py
@@ -83,7 +83,6 @@
     slot_index = jnp.arange(slot_count, dtype=jnp.int32)
     send_hot = slot[None, :] == slot_index[:, None]
     send_src = jnp.sum(jnp.where(send_hot, unit_index[None, :], 0), axis=1)
-    w_out_full = lax.all_gather(w_out, "tensor", axis=0, tiled=True)
     position = dest_row % units
     filled = jnp.any(send_hot, axis=1)
     slot_pos = jnp.where(filled, jnp.sum(jnp.where(send_hot, position[None, :], 0), axis=1), -1)
@@ -102,7 +101,10 @@
     pos_of_slot = jnp.maximum(recv_pos, 0)
     grouped = jnp.take(recv_units, slot_of_pos, axis=0, mode="clip")
     grouped = grouped.reshape(tok_grp, feat_part)
-    grouped, w_out_full = lax.optimization_barrier((grouped, w_out_full))
+    grouped, w_out = lax.optimization_barrier((grouped, w_out))
+    w_out_full = lax.all_to_all(
+        jnp.broadcast_to(w_out[None], (shards,) + w_out.shape), "tensor", 0, 0, tiled=True
+    ).reshape(shards * w_out.shape[0], w_out.shape[1])
     full = lax.all_gather(grouped, "tensor", axis=1, tiled=True)
     normed = rms_scale(full, attn_gain).astype(jnp.bfloat16)
     seg_row = seg_ids[0]

time: 305 us -> 357 us (1.17)
  waiting for transfers between devices: 172 us -> 231 us
  blocking collectives: 45.8 us -> 26.5 us
  starting transfers between devices: 6.86 us -> 15.8 us
    all_gather x1, waiting for transfers between devices: 53.1 us -> 87.2 us  [on_device(): full = lax.all_gather(grouped, 'tensor', axis=1, tiled=True)]
    all_to_all x0 -> x1, waiting for transfers between devices: none -> 23.1 us  [on_device(): lax.all_to_all(jnp.broadcast_to(w_out[None], (shards,) + w_out.shape), 't...]
    all_to_all x1, blocking collectives: 45.8 us -> 26.5 us  [on_device(): lax.all_to_all(payload, 'dp', split_axis=0, concat_axis=0, tiled=True)]
    all_gather x1, waiting for transfers between devices: 33.7 us -> 46.4 us  [on_device(): attended_full = lax.all_gather(attended, 'tensor', axis=1, tiled=True)]
    all_gather x1 -> x0, waiting for transfers between devices: 9.5 us -> none  [on_device(): w_out_full = lax.all_gather(w_out, 'tensor', axis=0, tiled=True)]
    all_to_all x0 -> x1, starting transfers between devices: none -> 8.89 us  [on_device(): lax.all_to_all(jnp.broadcast_to(w_out[None], (shards,) + w_out.shape), 't...]
  transfers between devices with their start and end apart: 5 -> 5, of which waited for: 5 -> 5; matrix products, arithmetic and copies ran while one was open for 5% -> 6% of each run, Pallas kernels for 0% -> 0%
where the time goes in v4:
time: 357 us
  waiting for transfers between devices  231 us (65%)
  matrix products  34.9 us (10%)
  blocking collectives  26.5 us (7%)
  local copies, waits for them, and re-layouts  20 us (6%)
  starting transfers between devices  15.8 us (4%)
  between operations  14.9 us (4%)
  other arithmetic  13 us (4%)
    all_gather x1, waiting for transfers between devices, on_device(): full = lax.all_gather(grouped, 'tensor', axis=1, tiled=True)  87.2 us
    reduce_scatter x1, waiting for transfers between devices, on_device(): lax.psum_scatter(jnp.dot(hidden, w_down, preferred_element_type=jnp.float...  59.3 us
    all_gather x1, waiting for transfers between devices, on_device(): attended_full = lax.all_gather(attended, 'tensor', axis=1, tiled=True)  46.4 us
    all_to_all x1, blocking collectives, on_device(): lax.all_to_all(payload, 'dp', split_axis=0, concat_axis=0, tiled=True)  26.5 us
    all_to_all x1, waiting for transfers between devices, on_device(): lax.all_to_all(jnp.broadcast_to(w_out[None], (shards,) + w_out.shape), 't...  23.1 us
    all_to_all x1, waiting for transfers between devices, on_device(): lax.all_to_all(back.reshape(groups, MOST, unit_rows, feat_part), 'dp', sp...  15.4 us
    dot_general x1, matrix products, on_device(): jnp.dot(hidden, w_down, preferred_element_type=jnp.float32)  12.3 us
    dot_general x1, matrix products, on_device(): jnp.dot(attended_full, w_out_full, preferred_element_type=jnp.float32)  9.41 us
  transfers between devices with their start and end apart: 5, of which 5 were waited for; matrix products, arithmetic and copies ran while one was open for 6% of the time, Pallas kernels for 0%

profile of v4, /device:TPU:65, one launch (start us, length us, event | category | flops | bytes accessed | tf_op | source)
XLA Modules:
  0.0 356.5 jit_solution(2916507668638920655)
XLA Ops:
  9.7 2.7 gather_fusion
  12.4 1.3 fusion.22
  13.7 26.5 %all_to_all.15 = bf16[32,72,256]{2,1,0:T(8,128)(2,1)S(1)} all-to-all(bf16[32,72,256]{2,1,0:T(8,128)(2,1)S(1)} %fusion.22), channel_id=1, replica_groups=mesh['dp'=32,'tensor'=8] {'dp'}, dimensions={0} | all-to-all | bytes 2359296 | tf_op jit(solution)/shard_map/all_to_all | solution.py:96
  41.6 2.4 slice.126
  43.9 2.6 gather_fusion.1
  51.4 2.5 broadcast_in_dim.126
  53.9 8.9 %all-to-all-start.1 = ((bf16[8,128,2048]{2,1,0:T(8,128)(2,1)}), bf16[8,128,2048]{2,1,0:T(8,128)(2,1)}, u32[]{:S(2)}, u32[]{:S(2)}) async-start(bf16[8,128,2048]{2,1,0:T(8,128)(2,1)} %broadcast_in_dim.126), calls=%async_computation.1 | async-start | bytes 8388608 | tf_op jit(solution)/shard_map/all_to_all | solution.py:105
  62.8 87.2 %all-gather.3.cloned.1.call-done = bf16[1024,2048]{1,0:T(8,128)(2,1)} async-done(((bf16[1024,256]{1,0:T(8,128)(2,1)}), bf16[1024,2048]{1,0:T(8,128)(2,1)}) %all-gather.3.cloned.1.call-update) | async-done | bytes 4194320 | tf_op jit(solution)/shard_map/all_gather | solution.py:108
  150.0 3.2 fusion.3
  153.5 2.6 fusion.20
  156.2 1.5 multiply_reduce_fusion
  161.4 1.3 fusion.23
  163.7 23.1 %all-to-all-done.1 = bf16[8,128,2048]{2,1,0:T(8,128)(2,1)} async-done(((bf16[8,128,2048]{2,1,0:T(8,128)(2,1)}), bf16[8,128,2048]{2,1,0:T(8,128)(2,1)}, u32[]{:S(2)}, u32[]{:S(2)}) %all-to-all-start.1) | async-done | bytes 4194336 | tf_op jit(solution)/shard_map/all_to_all | solution.py:105
  186.8 46.4 %all-gather.5.cloned.1.call-done = bf16[1024,1024]{0,1:T(8,128)(2,1)} async-done(((bf16[1024,128]{0,1:T(8,128)(2,1)}), bf16[1024,1024]{0,1:T(8,128)(2,1)}) %all-gather.5.cloned.1.call-update) | async-done | bytes 2097168 | tf_op jit(solution)/shard_map/all_gather | solution.py:161
  233.2 9.4 %fusion = (f32[1024]{0:T(1024)S(1)}, bf16[1024,2048]{1,0:T(8,128)(2,1)S(1)}) fusion(bf16[1024,1024]{0,1:T(8,128)(2,1)} %all-gather.5.cloned.1.call-done, bf16[1024,2048]{1,0:T(8,128)(2,1)} %bitcast.40, bf16[1024,2048]{1,0:T(8,128)(2,1)} %all-gather.3.cloned.1.call-done), kind=kOutput, calls=%fused_computation.10 | convolution fusion | flops 4307549184 | bytes 14684160 | tf_op jit(solution)/shard_map/dot_general | solution.py:162
  242.7 1.9 copy-done.11
  244.6 5.1 %fusion.14 = f32[1024,640]{1,0:T(8,128)} fusion(bf16[2048,640]{1,0:T(8,128)(2,1)S(1)} %copy-done.19, bf16[1024,2048]{1,0:T(8,128)(2,1)S(1)} %get-tuple-element.41, f32[2048]{0:T(1024)S(1)} %copy-done.22, f32[1024]{0:T(1024)S(1)} %add_rsqrt_fusion.1), kind=kOutput, calls=%fused_computation.32 | convolution fusion | flops 2692743168 | bytes 9449472 | tf_op jit(solution)/shard_map/dot_general | solution.py:165
  249.6 12.3 %convolution_convert_fusion = bf16[1024,2048]{1,0:T(8,128)(2,1)} fusion(bf16[640,2048]{1,0:T(8,128)(2,1)S(1)} %copy-done, f32[1024,640]{1,0:T(8,128)} %fusion.14, bf16[2048,640]{1,0:T(8,128)(2,1)} %param.28, bf16[1024,2048]{1,0:T(8,128)(2,1)} %copy-done.11, f32[2048]{0:T(1024)S(1)} %copy-done.22, f32[1024]{0:T(1024)S(1)} %add_rsqrt_fusion.1), kind=kOutput, calls=%fused_computation.19 | convolution fusion | flops 5383127040 | bytes 16265216 | tf_op jit(solution)/shard_map/dot_general | solution.py:169
  262.1 59.3 %reduce-scatter.2.cloned.1.call-done = bf16[1024,256]{1,0:T(8,128)(2,1)} async-done(((bf16[1024,2048]{1,0:T(8,128)(2,1)}), bf16[1024,256]{1,0:T(8,128)(2,1)}) %reduce-scatter.2.cloned.1.call-update) | async-done | bytes 524304 | tf_op jit(solution)/shard_map/reduce_scatter | solution.py:168
  321.4 1.3 add_convert_fusion
  322.7 1.6 gather_fusion.2
  324.4 6.6 %all-to-all-start.2 = ((bf16[32,2,32,256]{3,2,1,0:T(8,128)(2,1)}), bf16[32,2,32,256]{3,2,1,0:T(8,128)(2,1)}, u32[]{:S(2)}, u32[]{:S(2)}) async-start(bf16[32,2,32,256]{3,2,1,0:T(8,128)(2,1)} %bitcast.155), calls=%async_computation.3 | async-start | bytes 2097152 | tf_op jit(solution)/shard_map/all_to_all | solution.py:177
  331.9 15.4 %all-to-all-done.2 = bf16[32,2,32,256]{3,2,1,0:T(8,128)(2,1)} async-done(((bf16[32,2,32,256]{3,2,1,0:T(8,128)(2,1)}), bf16[32,2,32,256]{3,2,1,0:T(8,128)(2,1)}, u32[]{:S(2)}, u32[]{:S(2)}) %all-to-all-start.2) | async-done | bytes 1048608 | tf_op jit(solution)/shard_map/all_to_all | solution.py:177
  347.4 2.6 gather_fusion.3
  (111 shorter events, 13.7 us)
Async XLA Ops:
  7.2 242.5 %copy-start = (bf16[640,2048]{1,0:T(8,128)(2,1)S(1)}, bf16[640,2048]{1,0:T(8,128)(2,1)}, u32[]{:S(2)}) copy-start(bf16[640,2048]{1,0:T(8,128)(2,1)} %param.29) | copy-start | bytes 7864324
  7.2 142.8 %all-gather.3.cloned.1.call-start = ((), (), s32[]{:S(2)}) async-start(), calls=%async_computation.4 | async-start | bytes 4718592 | tf_op jit(solution)/shard_map/all_gather | solution.py:108
  12.4 34.2 %copy-start.14 = (s32[1,1024]{1,0:T(1,128)S(1)}, s32[1,1024]{1,0:T(1,128)}, u32[]{:S(2)}) copy-start(s32[1,1024]{1,0:T(1,128)} %param.18) | copy-start | bytes 12292
  13.7 37.7 %copy-start.4 = (bf16[128,2048]{1,0:T(8,128)(2,1)S(1)}, bf16[128,2048]{1,0:T(8,128)(2,1)}, u32[]{:S(2)}) copy-start(bf16[128,2048]{1,0:T(8,128)(2,1)} %param.25) | copy-start | bytes 1572868
  48.3 5.6 %copy-start.15 = (f32[32]{0:T(128)}, f32[32]{0:T(128)S(1)}, u32[]{:S(2)}) copy-start(f32[32]{0:T(128)S(1)} %multiply_power_fusion) | copy-start | bytes 388
  48.5 5.4 %copy-start.12 = (f32[1024]{0:T(1024)}, f32[1024]{0:T(1024)S(1)}, u32[]{:S(2)}) copy-start(f32[1024]{0:T(1024)S(1)} %get-tuple-element.22) | copy-start | bytes 12292
  53.9 132.9 %all-to-all-start.1 = ((bf16[8,128,2048]{2,1,0:T(8,128)(2,1)}), bf16[8,128,2048]{2,1,0:T(8,128)(2,1)}, u32[]{:S(2)}, u32[]{:S(2)}) async-start(bf16[8,128,2048]{2,1,0:T(8,128)(2,1)} %broadcast_in_dim.126), calls=%async_computation.1 | async-start | bytes 8388608 | tf_op jit(solution)/shard_map/all_to_all | solution.py:105
  62.8 90.5 %copy-start.21 = (f32[2048]{0:T(1024)S(1)}, f32[2048]{0:T(1024)}, u32[]{:S(2)}) copy-start(f32[2048]{0:T(1024)} %param.20) | copy-start | bytes 24580
  62.8 170.4 %all-gather.5.cloned.1.call-start = ((), (), s32[]{:S(2)}) async-start(), calls=%async_computation.5 | async-start | bytes 2359296 | tf_op jit(solution)/shard_map/all_gather | solution.py:161
  150.0 3.4 copy-start.2
  153.5 2.7 copy-start.20
  156.2 2.3 copy-start.18
  156.2 2.5 copy-start.6
  158.5 2.2 copy-start.7
  163.5 157.9 %reduce-scatter.2.cloned.1.call-start = ((), (), s32[]{:S(2)}) async-start(), calls=%async_computation.6 | async-start | bytes 4718592 | tf_op jit(solution)/shard_map/reduce_scatter | solution.py:168
  233.2 11.3 %copy-start.19 = (bf16[2048,640]{1,0:T(8,128)(2,1)S(1)}, bf16[2048,640]{1,0:T(8,128)(2,1)}, u32[]{:S(2)}) copy-start(bf16[2048,640]{1,0:T(8,128)(2,1)} %param.27) | copy-start | bytes 7864324
  233.2 11.3 %copy-start.22 = (f32[2048]{0:T(1024)S(1)}, f32[2048]{0:T(1024)}, u32[]{:S(2)}) copy-start(f32[2048]{0:T(1024)} %param.26) | copy-start | bytes 24580
  261.9 69.0 %copy-start.23 = (s32[1,32]{1,0:T(1,128)S(1)}, s32[1,32]{1,0:T(1,128)}, u32[]{:S(2)}) copy-start(s32[1,32]{1,0:T(1,128)} %param.17) | copy-start | bytes 388
  261.9 69.1 %copy-start.26 = (s32[32]{0:T(128)S(1)}, s32[32]{0:T(128)}, u32[]{:S(2)}) copy-start(s32[32]{0:T(128)} %copy-done.25) | copy-start | bytes 388
  261.9 69.1 %copy-start.24 = (s32[1,8]{1,0:T(1,128)S(1)}, s32[1,8]{1,0:T(1,128)}, u32[]{:S(2)}) copy-start(s32[1,8]{1,0:T(1,128)} %param.19) | copy-start | bytes 100
  261.9 69.1 %copy-start.8 = (bf16[1024,1,32]{0,2,1:T(8,128)(2,1)S(1)}, bf16[1024,1,32]{0,2,1:T(8,128)(2,1)}, u32[]{:S(2)}) copy-start(bf16[1024,1,32]{0,2,1:T(8,128)(2,1)} %copy-done.7) | copy-start | bytes 196612
  262.0 69.1 %copy-start.10 = (bf16[1024,1,32]{0,2,1:T(8,128)(2,1)S(1)}, bf16[1024,1,32]{0,2,1:T(8,128)(2,1)}, u32[]{:S(2)}) copy-start(bf16[1024,1,32]{0,2,1:T(8,128)(2,1)} %copy-done.9) | copy-start | bytes 196612
  324.4 23.0 %all-to-all-start.2 = ((bf16[32,2,32,256]{3,2,1,0:T(8,128)(2,1)}), bf16[32,2,32,256]{3,2,1,0:T(8,128)(2,1)}, u32[]{:S(2)}, u32[]{:S(2)}) async-start(bf16[32,2,32,256]{3,2,1,0:T(8,128)(2,1)} %bitcast.155), calls=%async_computation.3 | async-start | bytes 2097152 | tf_op jit(solution)/shard_map/all_to_all | solution.py:177
  331.9 18.1 %copy-start.3 = (bf16[8,128,64]{1,2,0:T(8,128)(2,1)}, bf16[8,128,64]{1,2,0:T(8,128)(2,1)S(1)}, u32[]{:S(2)}) copy-start(bf16[8,128,64]{1,2,0:T(8,128)(2,1)S(1)} %scatter_fusion) | copy-start | bytes 393220
  (8 other events, 12.5 us)
Sparse Core Ops, SparseCore 0:
  46.7 103.2 all-gather.2
  163.6 69.5 all-gather.4
  262.1 59.2 reduce-scatter.1

commit v5 on v3

--- a/solution.py
+++ b/solution.py
@@ -83,7 +83,8 @@
     slot_index = jnp.arange(slot_count, dtype=jnp.int32)
     send_hot = slot[None, :] == slot_index[:, None]
     send_src = jnp.sum(jnp.where(send_hot, unit_index[None, :], 0), axis=1)
-    w_out_full = lax.all_gather(w_out, "tensor", axis=0, tiled=True)
+    early_rows = w_out.shape[0] * 3 // 4
+    w_out_early = lax.all_gather(w_out[:early_rows], "tensor", axis=0, tiled=False)
     position = dest_row % units
     filled = jnp.any(send_hot, axis=1)
     slot_pos = jnp.where(filled, jnp.sum(jnp.where(send_hot, position[None, :], 0), axis=1), -1)
@@ -102,8 +103,13 @@
     pos_of_slot = jnp.maximum(recv_pos, 0)
     grouped = jnp.take(recv_units, slot_of_pos, axis=0, mode="clip")
     grouped = grouped.reshape(tok_grp, feat_part)
-    grouped, w_out_full = lax.optimization_barrier((grouped, w_out_full))
+    grouped, w_out_early = lax.optimization_barrier((grouped, w_out_early))
     full = lax.all_gather(grouped, "tensor", axis=1, tiled=True)
+    full, w_out_late = lax.optimization_barrier((full, w_out[early_rows:]))
+    w_out_late = lax.all_gather(w_out_late, "tensor", axis=0, tiled=False)
+    w_out_full = jnp.concatenate([w_out_early, w_out_late], axis=1).reshape(
+        shards * w_out.shape[0], w_out.shape[1]
+    )
     normed = rms_scale(full, attn_gain).astype(jnp.bfloat16)
     seg_row = seg_ids[0]
     starts = segment_starts(seg_row)

time: 305 us -> 325 us (1.066)
  other arithmetic: 12.6 us -> 20.2 us
  waiting for transfers between devices: 172 us -> 177 us
  local copies, waits for them, and re-layouts: 17.9 us -> 21.4 us
    all_gather x1 -> x2, waiting for transfers between devices: 9.5 us -> 16.1 us  [the longest x1 16.1 us: on_device(): w_out_late = lax.all_gather(w_out_late, 'tensor', axis=0, tiled=False)]
    concatenate x0 -> x1, other arithmetic: none -> 4.77 us  [on_device(): jnp.concatenate([w_out_early, w_out_late], axis=1)]
    slice x0 -> x2, local copies, waits for them, and re-layouts: none -> 3.49 us  [the longest x1 1.92 us: on_device(): w_out[:early_rows]]
  transfers between devices with their start and end apart: 5 -> 6, of which waited for: 5 -> 5; matrix products, arithmetic and copies ran while one was open for 5% -> 10% of each run, Pallas kernels for 0% -> 0%
where the time goes in v5:
time: 325 us; the launch traced here: 324 us
  waiting for transfers between devices  177 us (54%)
  blocking collectives  46.3 us (14%)
  matrix products  37.2 us (11%)
  local copies, waits for them, and re-layouts  21.4 us (7%)
  other arithmetic  20.2 us (6%)
  between operations  14.9 us (5%)
  starting transfers between devices  6.99 us (2%)
    reduce_scatter x1, waiting for transfers between devices, on_device(): lax.psum_scatter(jnp.dot(hidden, w_down, preferred_element_type=jnp.float...  59.3 us
    all_gather x1, waiting for transfers between devices, on_device(): full = lax.all_gather(grouped, 'tensor', axis=1, tiled=True)  55 us
    all_to_all x1, blocking collectives, on_device(): lax.all_to_all(payload, 'dp', split_axis=0, concat_axis=0, tiled=True)  46.3 us
    all_gather x1, waiting for transfers between devices, on_device(): attended_full = lax.all_gather(attended, 'tensor', axis=1, tiled=True)  31.6 us
    all_gather x1, waiting for transfers between devices, on_device(): w_out_late = lax.all_gather(w_out_late, 'tensor', axis=0, tiled=False)  16.1 us
    all_to_all x1, waiting for transfers between devices, on_device(): lax.all_to_all(back.reshape(groups, MOST, unit_rows, feat_part), 'dp', sp...  15.4 us
    dot_general x1, matrix products, on_device(): jnp.dot(hidden, w_down, preferred_element_type=jnp.float32)  12.3 us
    dot_general x1, matrix products, on_device(): jnp.dot(attended_full, w_out_full, preferred_element_type=jnp.float32)  9.41 us
  transfers between devices with their start and end apart: 6, of which 5 were waited for; matrix products, arithmetic and copies ran while one was open for 10% of the time, Pallas kernels for 0%

profile of v5, /device:TPU:65, one launch (start us, length us, event | category | flops | bytes accessed | tf_op | source)
XLA Modules:
  0.0 324.3 jit_solution(12779263910510892866)
XLA Ops:
  7.2 1.9 slice.105
  11.5 2.6 gather_fusion
  14.2 1.3 fusion.22
  15.5 46.3 %all_to_all.10 = bf16[32,72,256]{2,1,0:T(8,128)(2,1)S(1)} all-to-all(bf16[32,72,256]{2,1,0:T(8,128)(2,1)S(1)} %fusion.22), channel_id=1, replica_groups=mesh['dp'=32,'tensor'=8] {'dp'}, dimensions={0} | all-to-all | bytes 2359296 | tf_op jit(solution)/shard_map/all_to_all | solution.py:98
  63.0 2.4 slice.134
  65.5 2.6 gather_fusion.1
  68.2 1.6 slice.106
  75.0 55.0 %all-gather.7.cloned.1.call-done = bf16[1024,2048]{1,0:T(8,128)(2,1)} async-done(((bf16[1024,256]{1,0:T(8,128)(2,1)}), bf16[1024,2048]{1,0:T(8,128)(2,1)}) %all-gather.7.cloned.1.call-update) | async-done | bytes 4194320 | tf_op jit(solution)/shard_map/all_gather | solution.py:107
  130.1 3.2 fusion.3
  133.5 2.6 fusion.20
  139.5 3.9 %multiply_reduce_fusion = (f32[1024,2]{0,1:T(2,128)S(1)}, f32[1024,128]{0,1:T(8,128)S(1)}) fusion(bf16[2048,128]{1,0:T(8,128)(2,1)} %param.21, bf16[1024,2048]{1,0:T(8,128)(2,1)} %all-gather.7.cloned.1.call-done, f32[2048]{0:T(1024)} %param.20, f32[1024]{0:T(1024)} %copy-done.13), kind=kOutput, calls=%fused_computation.43 | convolution fusion | flops 545519616 | bytes 5263360 | tf_op jit(solution)/shard_map/dot_general | solution.py:119
  148.7 16.1 %all-gather.13.cloned.1.call-done = bf16[256,2048]{1,0:T(8,128)(2,1)} async-done(((bf16[32,2048]{1,0:T(8,128)(2,1)}), bf16[256,2048]{1,0:T(8,128)(2,1)}) %all-gather.13.cloned.1.call-update) | async-done | bytes 1048592 | tf_op jit(solution)/shard_map/all_gather | solution.py:109
  164.7 4.8 %pad_maximum_fusion = bf16[8,128,2048]{2,1,0:T(8,128)(2,1)} fusion(bf16[8,32,2048]{2,1,0:T(8,128)(2,1)} %bitcast.164, bf16[8,96,2048]{2,1,0:T(8,128)(2,1)} %bitcast.160), kind=kLoop, calls=%fused_computation.17 | loop fusion | flops 8388608 | bytes 8388608 | tf_op jit(solution)/shard_map/concatenate | solution.py:110
  169.5 31.6 %all-gather.9.cloned.1.call-done = bf16[1024,1024]{0,1:T(8,128)(2,1)} async-done(((bf16[1024,128]{0,1:T(8,128)(2,1)}), bf16[1024,1024]{0,1:T(8,128)(2,1)}) %all-gather.9.cloned.1.call-update) | async-done | bytes 2097168 | tf_op jit(solution)/shard_map/all_gather | solution.py:165
  201.1 9.4 %fusion = (f32[1024]{0:T(1024)S(1)}, bf16[1024,2048]{1,0:T(8,128)(2,1)S(1)}) fusion(bf16[1024,1024]{0,1:T(8,128)(2,1)} %all-gather.9.cloned.1.call-done, bf16[1024,2048]{1,0:T(8,128)(2,1)} %bitcast.159, bf16[1024,2048]{1,0:T(8,128)(2,1)} %all-gather.7.cloned.1.call-done), kind=kOutput, calls=%fused_computation.10 | convolution fusion | flops 4307549184 | bytes 14684160 | tf_op jit(solution)/shard_map/dot_general | solution.py:166
  210.5 1.9 copy-done.10
  212.5 5.1 %fusion.14 = f32[1024,640]{1,0:T(8,128)} fusion(bf16[2048,640]{1,0:T(8,128)(2,1)S(1)} %copy-done.16, bf16[1024,2048]{1,0:T(8,128)(2,1)S(1)} %get-tuple-element.45, f32[2048]{0:T(1024)S(1)} %copy-done.18, f32[1024]{0:T(1024)S(1)} %add_rsqrt_fusion.1), kind=kOutput, calls=%fused_computation.33 | convolution fusion | flops 2692743168 | bytes 9449472 | tf_op jit(solution)/shard_map/dot_general | solution.py:169
  217.5 12.3 %convolution_convert_fusion = bf16[1024,2048]{1,0:T(8,128)(2,1)} fusion(bf16[640,2048]{1,0:T(8,128)(2,1)S(1)} %copy-done, f32[1024,640]{1,0:T(8,128)} %fusion.14, bf16[2048,640]{1,0:T(8,128)(2,1)} %param.28, bf16[1024,2048]{1,0:T(8,128)(2,1)} %copy-done.10, f32[2048]{0:T(1024)S(1)} %copy-done.18, f32[1024]{0:T(1024)S(1)} %add_rsqrt_fusion.1), kind=kOutput, calls=%fused_computation.20 | convolution fusion | flops 5383127040 | bytes 16265216 | tf_op jit(solution)/shard_map/dot_general | solution.py:173
  230.0 59.3 %reduce-scatter.2.cloned.1.call-done = bf16[1024,256]{1,0:T(8,128)(2,1)} async-done(((bf16[1024,2048]{1,0:T(8,128)(2,1)}), bf16[1024,256]{1,0:T(8,128)(2,1)}) %reduce-scatter.2.cloned.1.call-update) | async-done | bytes 524304 | tf_op jit(solution)/shard_map/reduce_scatter | solution.py:172
  289.3 1.3 add_convert_fusion
  290.6 1.6 gather_fusion.2
  292.2 6.6 %all-to-all-start.1 = ((bf16[32,2,32,256]{3,2,1,0:T(8,128)(2,1)}), bf16[32,2,32,256]{3,2,1,0:T(8,128)(2,1)}, u32[]{:S(2)}, u32[]{:S(2)}) async-start(bf16[32,2,32,256]{3,2,1,0:T(8,128)(2,1)} %bitcast.157), calls=%async_computation.2 | async-start | bytes 2097152 | tf_op jit(solution)/shard_map/all_to_all | solution.py:181
  299.8 15.4 %all-to-all-done.1 = bf16[32,2,32,256]{3,2,1,0:T(8,128)(2,1)} async-done(((bf16[32,2,32,256]{3,2,1,0:T(8,128)(2,1)}), bf16[32,2,32,256]{3,2,1,0:T(8,128)(2,1)}, u32[]{:S(2)}, u32[]{:S(2)}) %all-to-all-start.1) | async-done | bytes 1048608 | tf_op jit(solution)/shard_map/all_to_all | solution.py:181
  315.2 2.6 gather_fusion.3
  (109 shorter events, 18.1 us)
Async XLA Ops:
  7.2 210.4 %copy-start = (bf16[640,2048]{1,0:T(8,128)(2,1)S(1)}, bf16[640,2048]{1,0:T(8,128)(2,1)}, u32[]{:S(2)}) copy-start(bf16[640,2048]{1,0:T(8,128)(2,1)} %param.29) | copy-start | bytes 7864324
  7.2 60.9 %all-gather.11.cloned.1.call-start = ((), (), s32[]{:S(2)}) async-start(), calls=%async_computation.6 | async-start | bytes 3538944 | tf_op jit(solution)/shard_map/all_gather | solution.py:87
  9.2 120.9 %all-gather.7.cloned.1.call-start = ((), (), s32[]{:S(2)}) async-start(), calls=%async_computation.3 | async-start | bytes 4718592 | tf_op jit(solution)/shard_map/all_gather | solution.py:107
  14.2 55.6 %copy-start.12 = (s32[1,1024]{1,0:T(1,128)S(1)}, s32[1,1024]{1,0:T(1,128)}, u32[]{:S(2)}) copy-start(s32[1,1024]{1,0:T(1,128)} %param.18) | copy-start | bytes 12292
  63.0 70.3 %copy-start.17 = (f32[2048]{0:T(1024)S(1)}, f32[2048]{0:T(1024)}, u32[]{:S(2)}) copy-start(f32[2048]{0:T(1024)} %param.20) | copy-start | bytes 24580
  68.1 96.6 %all-gather.13.cloned.1.call-start = ((), (), s32[]{:S(2)}) async-start(), calls=%async_computation.7 | async-start | bytes 1179648 | tf_op jit(solution)/shard_map/all_gather | solution.py:109
  71.4 61.9 %copy-start.14 = (f32[32]{0:T(128)}, f32[32]{0:T(128)S(1)}, u32[]{:S(2)}) copy-start(f32[32]{0:T(128)S(1)} %multiply_power_fusion) | copy-start | bytes 388
  130.1 3.4 %copy-start.2 = (bf16[1024,2048]{1,0:T(8,128)(2,1)S(1)}, bf16[1024,2048]{1,0:T(8,128)(2,1)}, u32[]{:S(2)}) copy-start(bf16[1024,2048]{1,0:T(8,128)(2,1)} %all-gather.7.cloned.1.call-done) | copy-start | bytes 12582916
  133.5 2.6 copy-start.13
  136.8 64.3 %all-gather.9.cloned.1.call-start = ((), (), s32[]{:S(2)}) async-start(), calls=%async_computation.4 | async-start | bytes 2359296 | tf_op jit(solution)/shard_map/all_gather | solution.py:165
  139.5 5.0 %copy-start.6 = (bf16[1024,1,32]{0,2,1:T(8,128)(2,1)}, bf16[1024,1,32]{0,2,1:T(8,128)(2,1)S(1)}, u32[]{:S(2)}) copy-start(bf16[1024,1,32]{0,2,1:T(8,128)(2,1)S(1)} %get-tuple-element.30) | copy-start | bytes 196612
  139.5 5.0 %copy-start.8 = (bf16[1024,1,32]{0,2,1:T(8,128)(2,1)}, bf16[1024,1,32]{0,2,1:T(8,128)(2,1)S(1)}, u32[]{:S(2)}) copy-start(bf16[1024,1,32]{0,2,1:T(8,128)(2,1)S(1)} %get-tuple-element.31) | copy-start | bytes 196612
  139.5 4.0 %copy-start.15 = (f32[64]{0:T(128)S(1)}, f32[64]{0:T(128)}, u32[]{:S(2)}) copy-start(f32[64]{0:T(128)} %param.23) | copy-start | bytes 772
  139.5 4.2 %copy-start.5 = (pred[512,512]{0,1:T(8,128)(4,1)S(1)}, pred[512,512]{0,1:T(8,128)(4,1)}, u32[]{:S(2)}) copy-start(pred[512,512]{0,1:T(8,128)(4,1)} %compare_and_fusion) | copy-start | bytes 786436
  148.4 140.8 %reduce-scatter.2.cloned.1.call-start = ((), (), s32[]{:S(2)}) async-start(), calls=%async_computation.5 | async-start | bytes 4718592 | tf_op jit(solution)/shard_map/reduce_scatter | solution.py:172
  201.1 11.4 %copy-start.16 = (bf16[2048,640]{1,0:T(8,128)(2,1)S(1)}, bf16[2048,640]{1,0:T(8,128)(2,1)}, u32[]{:S(2)}) copy-start(bf16[2048,640]{1,0:T(8,128)(2,1)} %param.27) | copy-start | bytes 7864324
  201.1 11.4 %copy-start.18 = (f32[2048]{0:T(1024)S(1)}, f32[2048]{0:T(1024)}, u32[]{:S(2)}) copy-start(f32[2048]{0:T(1024)} %param.26) | copy-start | bytes 24580
  229.8 69.0 %copy-start.19 = (s32[1,32]{1,0:T(1,128)S(1)}, s32[1,32]{1,0:T(1,128)}, u32[]{:S(2)}) copy-start(s32[1,32]{1,0:T(1,128)} %param.17) | copy-start | bytes 388
  229.8 69.1 %copy-start.22 = (s32[32]{0:T(128)S(1)}, s32[32]{0:T(128)}, u32[]{:S(2)}) copy-start(s32[32]{0:T(128)} %copy-done.21) | copy-start | bytes 388
  229.8 69.1 %copy-start.20 = (s32[1,8]{1,0:T(1,128)S(1)}, s32[1,8]{1,0:T(1,128)}, u32[]{:S(2)}) copy-start(s32[1,8]{1,0:T(1,128)} %param.19) | copy-start | bytes 100
  229.8 69.1 %copy-start.7 = (bf16[1024,1,32]{0,2,1:T(8,128)(2,1)S(1)}, bf16[1024,1,32]{0,2,1:T(8,128)(2,1)}, u32[]{:S(2)}) copy-start(bf16[1024,1,32]{0,2,1:T(8,128)(2,1)} %copy-done.6) | copy-start | bytes 196612
  229.8 69.1 %copy-start.9 = (bf16[1024,1,32]{0,2,1:T(8,128)(2,1)S(1)}, bf16[1024,1,32]{0,2,1:T(8,128)(2,1)}, u32[]{:S(2)}) copy-start(bf16[1024,1,32]{0,2,1:T(8,128)(2,1)} %copy-done.8) | copy-start | bytes 196612
  292.2 23.0 %all-to-all-start.1 = ((bf16[32,2,32,256]{3,2,1,0:T(8,128)(2,1)}), bf16[32,2,32,256]{3,2,1,0:T(8,128)(2,1)}, u32[]{:S(2)}, u32[]{:S(2)}) async-start(bf16[32,2,32,256]{3,2,1,0:T(8,128)(2,1)} %bitcast.157), calls=%async_computation.2 | async-start | bytes 2097152 | tf_op jit(solution)/shard_map/all_to_all | solution.py:181
  299.8 18.0 %copy-start.3 = (bf16[8,128,64]{1,2,0:T(8,128)(2,1)}, bf16[8,128,64]{1,2,0:T(8,128)(2,1)S(1)}, u32[]{:S(2)}) copy-start(bf16[8,128,64]{1,2,0:T(8,128)(2,1)S(1)} %scatter_fusion) | copy-start | bytes 393220
  (5 other events, 5.1 us)
Sparse Core Ops, SparseCore 0:
  10.4 54.0 all-gather.10
  68.2 61.7 all-gather.6
  136.9 27.8 all-gather.12
  167.0 34.0 all-gather.8
  230.0 59.2 reduce-scatter.1

commit v6 on v3

--- a/solution.py
+++ b/solution.py
@@ -110,16 +110,15 @@
     index = jnp.arange(tok_grp, dtype=jnp.int32)
     cosine, sine = rope_tables(index - starts, HEAD)
     q_heads = w_query.shape[1] // HEAD
-    q_raw = jnp.dot(normed, w_query, preferred_element_type=jnp.float32).reshape(
-        tok_grp, q_heads, HEAD
-    )
-    queries = rotate(rms_scale(q_raw, query_gain), cosine, sine).astype(jnp.bfloat16)
     kv_heads = max(1, KVH // shards)
     kv_first = tensor_rank * KVH // shards
     kv_weight = lax.dynamic_slice_in_dim(w_keyval, kv_first * 2 * HEAD, kv_heads * 2 * HEAD, 1)
-    kv_raw = jnp.dot(normed, kv_weight, preferred_element_type=jnp.float32).reshape(
-        tok_grp, kv_heads, 2, HEAD
-    )
+    qkv_weight = jnp.concatenate([w_query, kv_weight], axis=1)
+    qkv_raw = jnp.dot(normed, qkv_weight, preferred_element_type=jnp.float32)
+    q_cols = w_query.shape[1]
+    q_raw = qkv_raw[:, :q_cols].reshape(tok_grp, q_heads, HEAD)
+    queries = rotate(rms_scale(q_raw, query_gain), cosine, sine).astype(jnp.bfloat16)
+    kv_raw = qkv_raw[:, q_cols:].reshape(tok_grp, kv_heads, 2, HEAD)
     keys = rotate(rms_scale(kv_raw[:, :, 0], key_gain), cosine, sine).astype(jnp.bfloat16)
     values = kv_raw[:, :, 1].astype(jnp.bfloat16)
     stacked = jnp.stack([keys, values], axis=2).reshape(tok_grp, kv_heads * 2 * HEAD)
@@ -160,8 +159,12 @@
     attn_sum = jnp.dot(attended_full, w_out_full, preferred_element_type=jnp.float32)
     middle = (full.astype(jnp.float32) + attn_sum).astype(jnp.bfloat16)
     ffn_in = rms_scale(middle, ffn_gain).astype(jnp.bfloat16)
-    gate = jnp.dot(ffn_in, w_gate, preferred_element_type=jnp.float32)
-    upper = jnp.dot(ffn_in, w_up, preferred_element_type=jnp.float32)
+    ff_part = w_gate.shape[1]
+    gate_up = jnp.dot(
+        ffn_in, jnp.concatenate([w_gate, w_up], axis=1), preferred_element_type=jnp.float32
+    )
+    gate = gate_up[:, :ff_part]
+    upper = gate_up[:, ff_part:]
     hidden = (jax.nn.silu(gate) * upper).astype(jnp.bfloat16)
     ffn_part = lax.psum_scatter(
         jnp.dot(hidden, w_down, preferred_element_type=jnp.float32).astype(jnp.bfloat16),

time: 305 us -> 295 us (0.967)
  matrix products: 34.9 us -> 26.8 us
    dot_general x1, matrix products: 12.3 us -> 5.07 us  [on_device(): jnp.dot(hidden, w_down, preferred_element_type=jnp.float32)]
    dot_general x3 -> x2, matrix products: 9.25 us -> 8.41 us  [the longest x1 5.66 us: on_device(): jnp.dot(ffn_in, jnp.concatenate([w_gate, w_up], axis=1), preferred_elemen...]
  transfers between devices with their start and end apart: 5 -> 5, of which waited for: 5 -> 5; matrix products, arithmetic and copies ran while one was open for 5% -> 6% of each run, Pallas kernels for 0% -> 0%
where the time goes in v6:
time: 295 us; the launch traced here: 294 us
  waiting for transfers between devices  169 us (57%)
  blocking collectives  45.8 us (16%)
  matrix products  26.8 us (9%)
  local copies, waits for them, and re-layouts  18 us (6%)
  between operations  14.9 us (5%)
  other arithmetic  12.7 us (4%)
  starting transfers between devices  6.97 us (2%)
    reduce_scatter x1, waiting for transfers between devices, on_device(): lax.psum_scatter(jnp.dot(hidden, w_down, preferred_element_type=jnp.float...  59.2 us
    all_gather x1, waiting for transfers between devices, on_device(): full = lax.all_gather(grouped, 'tensor', axis=1, tiled=True)  51.1 us
    all_to_all x1, blocking collectives, on_device(): lax.all_to_all(payload, 'dp', split_axis=0, concat_axis=0, tiled=True)  45.8 us
    all_gather x1, waiting for transfers between devices, on_device(): attended_full = lax.all_gather(attended, 'tensor', axis=1, tiled=True)  33.3 us
    all_to_all x1, waiting for transfers between devices, on_device(): lax.all_to_all(back.reshape(groups, MOST, unit_rows, feat_part), 'dp', sp...  15.4 us
    all_gather x1, waiting for transfers between devices, on_device(): w_out_full = lax.all_gather(w_out, 'tensor', axis=0, tiled=True)  9.52 us
    dot_general x1, matrix products, on_device(): jnp.dot(attended_full, w_out_full, preferred_element_type=jnp.float32)  9.41 us
    all_to_all x1, starting transfers between devices, on_device(): lax.all_to_all(back.reshape(groups, MOST, unit_rows, feat_part), 'dp', sp...  6.63 us
  transfers between devices with their start and end apart: 5, of which 5 were waited for; matrix products, arithmetic and copies ran while one was open for 6% of the time, Pallas kernels for 0%

profile of v6, /device:TPU:65, one launch (start us, length us, event | category | flops | bytes accessed | tf_op | source)
XLA Modules:
  0.0 294.5 jit_solution(16871469863724311265)
XLA Ops:
  10.2 2.6 gather_fusion
  12.9 1.3 fusion.27
  14.2 45.8 %all_to_all.10 = bf16[32,72,256]{2,1,0:T(8,128)(2,1)S(1)} all-to-all(bf16[32,72,256]{2,1,0:T(8,128)(2,1)S(1)} %fusion.27), channel_id=1, replica_groups=mesh['dp'=32,'tensor'=8] {'dp'}, dimensions={0} | all-to-all | bytes 2359296 | tf_op jit(solution)/shard_map/all_to_all | solution.py:97
  60.0 1.0 copy-done.1
  61.2 2.4 slice.142
  63.7 2.6 gather_fusion.1
  66.3 9.5 %all-gather.4.cloned.1.call-done = bf16[1024,2048]{1,0:T(8,128)(2,1)} async-done(((bf16[128,2048]{1,0:T(8,128)(2,1)}), bf16[1024,2048]{1,0:T(8,128)(2,1)}) %all-gather.4.cloned.1.call-update) | async-done | bytes 4194320 | tf_op jit(solution)/shard_map/all_gather | solution.py:86
  80.0 1.9 constant_dynamic-slice_fusion
  82.4 51.1 %all-gather.6.cloned.1.call-done = bf16[1024,2048]{1,0:T(8,128)(2,1)} async-done(((bf16[1024,256]{1,0:T(8,128)(2,1)}), bf16[1024,2048]{1,0:T(8,128)(2,1)}) %all-gather.6.cloned.1.call-update) | async-done | bytes 4194320 | tf_op jit(solution)/shard_map/all_gather | solution.py:106
  133.5 3.2 %fusion.3 = f32[1024]{0:T(1024)S(1)} fusion(bf16[1024,2048]{1,0:T(8,128)(2,1)} %all-gather.6.cloned.1.call-done), kind=kLoop, calls=%fused_computation.13 | loop fusion | flops 6290432 | bytes 4198400 | tf_op jit(solution)/shard_map/reduce_sum | solution.py:21
  137.0 2.7 fusion.11
  140.1 1.2 fusion.40
  142.2 1.1 fusion.18
  143.4 1.3 fusion.28
  146.5 33.3 %all-gather.8.cloned.1.call-done = bf16[1024,1024]{0,1:T(8,128)(2,1)} async-done(((bf16[1024,128]{0,1:T(8,128)(2,1)}), bf16[1024,1024]{0,1:T(8,128)(2,1)}) %all-gather.8.cloned.1.call-update) | async-done | bytes 2097168 | tf_op jit(solution)/shard_map/all_gather | solution.py:158
  179.7 9.4 %fusion = (f32[1024]{0:T(1024)S(1)}, bf16[1024,2048]{1,0:T(8,128)(2,1)S(1)}) fusion(bf16[1024,1024]{0,1:T(8,128)(2,1)} %all-gather.8.cloned.1.call-done, bf16[1024,2048]{1,0:T(8,128)(2,1)} %all-gather.4.cloned.1.call-done, bf16[1024,2048]{1,0:T(8,128)(2,1)} %all-gather.6.cloned.1.call-done), kind=kOutput, calls=%fused_computation.10 | convolution fusion | flops 4307549184 | bytes 14684160 | tf_op jit(solution)/shard_map/dot_general | solution.py:159
  189.2 5.7 %fusion.7 = f32[1024,1280]{1,0:T(8,128)S(1)} fusion(bf16[2048,640]{1,0:T(8,128)(2,1)S(1)} %copy-done.16, bf16[2048,640]{1,0:T(8,128)(2,1)S(1)} %copy-done.17, bf16[1024,2048]{1,0:T(8,128)(2,1)S(1)} %get-tuple-element.39, f32[2048]{0:T(1024)S(1)} %copy-done.19, f32[1024]{0:T(1024)S(1)} %add_rsqrt_fusion.1), kind=kOutput, calls=%fused_computation.17 | convolution fusion | flops 5387583488 | bytes 14692352 | tf_op jit(solution)/shard_map/dot_general | solution.py:163
  194.9 5.1 %convolution_convert_fusion = bf16[1024,2048]{1,0:T(8,128)(2,1)} fusion(bf16[640,2048]{1,0:T(8,128)(2,1)S(1)} %copy-done, f32[1024,1280]{1,0:T(8,128)S(1)} %fusion.7), kind=kOutput, calls=%fused_computation.28 | convolution fusion | flops 2690383872 | bytes 12058624 | tf_op jit(solution)/shard_map/dot_general | solution.py:170
  200.1 59.2 %reduce-scatter.2.cloned.1.call-done = bf16[1024,256]{1,0:T(8,128)(2,1)} async-done(((bf16[1024,2048]{1,0:T(8,128)(2,1)}), bf16[1024,256]{1,0:T(8,128)(2,1)}) %reduce-scatter.2.cloned.1.call-update) | async-done | bytes 524304 | tf_op jit(solution)/shard_map/reduce_scatter | solution.py:169
  259.4 1.3 add_convert_fusion
  260.7 1.6 gather_fusion.2
  262.3 6.6 %all-to-all-start.1 = ((bf16[32,2,32,256]{3,2,1,0:T(8,128)(2,1)}), bf16[32,2,32,256]{3,2,1,0:T(8,128)(2,1)}, u32[]{:S(2)}, u32[]{:S(2)}) async-start(bf16[32,2,32,256]{3,2,1,0:T(8,128)(2,1)} %bitcast.151), calls=%async_computation.2 | async-start | bytes 2097152 | tf_op jit(solution)/shard_map/all_to_all | solution.py:178
  269.9 15.4 %all-to-all-done.1 = bf16[32,2,32,256]{3,2,1,0:T(8,128)(2,1)} async-done(((bf16[32,2,32,256]{3,2,1,0:T(8,128)(2,1)}), bf16[32,2,32,256]{3,2,1,0:T(8,128)(2,1)}, u32[]{:S(2)}, u32[]{:S(2)}) %all-to-all-start.1) | async-done | bytes 1048608 | tf_op jit(solution)/shard_map/all_to_all | solution.py:178
  285.4 2.6 gather_fusion.3
  (107 shorter events, 11.4 us)
Async XLA Ops:
  7.2 187.7 %copy-start = (bf16[640,2048]{1,0:T(8,128)(2,1)S(1)}, bf16[640,2048]{1,0:T(8,128)(2,1)}, u32[]{:S(2)}) copy-start(bf16[640,2048]{1,0:T(8,128)(2,1)} %param.29) | copy-start | bytes 7864324
  7.2 68.7 %all-gather.4.cloned.1.call-start = ((), (), s32[]{:S(2)}) async-start(), calls=%async_computation.3 | async-start | bytes 4718592 | tf_op jit(solution)/shard_map/all_gather | solution.py:86
  7.9 125.6 %all-gather.6.cloned.1.call-start = ((), (), s32[]{:S(2)}) async-start(), calls=%async_computation.4 | async-start | bytes 4718592 | tf_op jit(solution)/shard_map/all_gather | solution.py:106
  12.9 63.0 %copy-start.12 = (s32[1,1024]{1,0:T(1,128)S(1)}, s32[1,1024]{1,0:T(1,128)}, u32[]{:S(2)}) copy-start(s32[1,1024]{1,0:T(1,128)} %param.18) | copy-start | bytes 12292
  63.6 73.2 %copy-start.18 = (f32[2048]{0:T(1024)S(1)}, f32[2048]{0:T(1024)}, u32[]{:S(2)}) copy-start(f32[2048]{0:T(1024)} %param.20) | copy-start | bytes 24580
  75.9 103.9 %all-gather.8.cloned.1.call-start = ((), (), s32[]{:S(2)}) async-start(), calls=%async_computation.5 | async-start | bytes 2359296 | tf_op jit(solution)/shard_map/all_gather | solution.py:158
  77.6 62.1 %copy-start.13 = (f32[32]{0:T(128)}, f32[32]{0:T(128)S(1)}, u32[]{:S(2)}) copy-start(f32[32]{0:T(128)S(1)} %multiply_power_fusion) | copy-start | bytes 388
  133.5 3.4 %copy-start.2 = (bf16[1024,2048]{1,0:T(8,128)(2,1)S(1)}, bf16[1024,2048]{1,0:T(8,128)(2,1)}, u32[]{:S(2)}) copy-start(bf16[1024,2048]{1,0:T(8,128)(2,1)} %all-gather.6.cloned.1.call-done) | copy-start | bytes 12582916
  137.0 3.0 %copy-start.14 = (f32[64]{0:T(128)S(1)}, f32[64]{0:T(128)}, u32[]{:S(2)}) copy-start(f32[64]{0:T(128)} %param.24) | copy-start | bytes 772
  137.0 3.1 %copy-start.11 = (f32[1024]{0:T(1024)S(1)}, f32[1024]{0:T(1024)}, u32[]{:S(2)}) copy-start(f32[1024]{0:T(1024)} %copy-done.10) | copy-start | bytes 12292
  137.0 4.3 %copy-start.15 = (f32[64]{0:T(128)S(1)}, f32[64]{0:T(128)}, u32[]{:S(2)}) copy-start(f32[64]{0:T(128)} %param.23) | copy-start | bytes 772
  141.3 2.1 copy-start.5
  146.2 43.0 %copy-start.19 = (f32[2048]{0:T(1024)S(1)}, f32[2048]{0:T(1024)}, u32[]{:S(2)}) copy-start(f32[2048]{0:T(1024)} %param.26) | copy-start | bytes 24580
  146.2 113.1 %reduce-scatter.2.cloned.1.call-start = ((), (), s32[]{:S(2)}) async-start(), calls=%async_computation.6 | async-start | bytes 4718592 | tf_op jit(solution)/shard_map/reduce_scatter | solution.py:169
  179.7 9.5 %copy-start.16 = (bf16[2048,640]{1,0:T(8,128)(2,1)S(1)}, bf16[2048,640]{1,0:T(8,128)(2,1)}, u32[]{:S(2)}) copy-start(bf16[2048,640]{1,0:T(8,128)(2,1)} %param.28) | copy-start | bytes 7864324
  179.7 9.5 %copy-start.17 = (bf16[2048,640]{1,0:T(8,128)(2,1)S(1)}, bf16[2048,640]{1,0:T(8,128)(2,1)}, u32[]{:S(2)}) copy-start(bf16[2048,640]{1,0:T(8,128)(2,1)} %param.27) | copy-start | bytes 7864324
  189.1 5.7 %copy-start.9 = (bf16[1024,2048]{1,0:T(8,128)(2,1)}, bf16[1024,2048]{1,0:T(8,128)(2,1)S(1)}, u32[]{:S(2)}) copy-start(bf16[1024,2048]{1,0:T(8,128)(2,1)S(1)} %get-tuple-element.39) | copy-start | bytes 12582916
  200.0 69.0 %copy-start.20 = (s32[1,32]{1,0:T(1,128)S(1)}, s32[1,32]{1,0:T(1,128)}, u32[]{:S(2)}) copy-start(s32[1,32]{1,0:T(1,128)} %param.17) | copy-start | bytes 388
  200.0 69.0 %copy-start.23 = (s32[32]{0:T(128)S(1)}, s32[32]{0:T(128)}, u32[]{:S(2)}) copy-start(s32[32]{0:T(128)} %copy-done.22) | copy-start | bytes 388
  200.0 69.1 %copy-start.21 = (s32[1,8]{1,0:T(1,128)S(1)}, s32[1,8]{1,0:T(1,128)}, u32[]{:S(2)}) copy-start(s32[1,8]{1,0:T(1,128)} %param.19) | copy-start | bytes 100
  200.0 69.1 %copy-start.6 = (bf16[1024,1,32]{0,2,1:T(8,128)(2,1)S(1)}, bf16[1024,1,32]{0,2,1:T(8,128)(2,1)}, u32[]{:S(2)}) copy-start(bf16[1024,1,32]{0,2,1:T(8,128)(2,1)} %copy-done.5) | copy-start | bytes 196612
  200.0 69.1 %copy-start.8 = (bf16[1024,1,32]{0,2,1:T(8,128)(2,1)S(1)}, bf16[1024,1,32]{0,2,1:T(8,128)(2,1)}, u32[]{:S(2)}) copy-start(bf16[1024,1,32]{0,2,1:T(8,128)(2,1)} %copy-done.7) | copy-start | bytes 196612
  262.3 23.0 %all-to-all-start.1 = ((bf16[32,2,32,256]{3,2,1,0:T(8,128)(2,1)}), bf16[32,2,32,256]{3,2,1,0:T(8,128)(2,1)}, u32[]{:S(2)}, u32[]{:S(2)}) async-start(bf16[32,2,32,256]{3,2,1,0:T(8,128)(2,1)} %bitcast.151), calls=%async_computation.2 | async-start | bytes 2097152 | tf_op jit(solution)/shard_map/all_to_all | solution.py:178
  269.9 18.0 %copy-start.3 = (bf16[8,128,64]{1,2,0:T(8,128)(2,1)}, bf16[8,128,64]{1,2,0:T(8,128)(2,1)S(1)}, u32[]{:S(2)}) copy-start(bf16[8,128,64]{1,2,0:T(8,128)(2,1)S(1)} %scatter_fusion) | copy-start | bytes 393220
  (5 other events, 6.0 us)
Sparse Core Ops, SparseCore 0:
  9.8 65.9 all-gather.3
  78.2 55.2 all-gather.5
  146.3 33.3 all-gather.7
  200.1 59.1 reduce-scatter.1

commit v7 on v6

--- a/solution.py
+++ b/solution.py
@@ -157,6 +157,7 @@
     attended = jnp.concatenate(outputs, axis=0)
     attended_full = lax.all_gather(attended, "tensor", axis=1, tiled=True)
     attn_sum = jnp.dot(attended_full, w_out_full, preferred_element_type=jnp.float32)
+    attn_sum = lax.optimization_barrier(attn_sum.astype(jnp.bfloat16)).astype(jnp.float32)
     middle = (full.astype(jnp.float32) + attn_sum).astype(jnp.bfloat16)
     ffn_in = rms_scale(middle, ffn_gain).astype(jnp.bfloat16)
     ff_part = w_gate.shape[1]
@@ -165,7 +166,7 @@
     )
     gate = gate_up[:, :ff_part]
     upper = gate_up[:, ff_part:]
-    hidden = (jax.nn.silu(gate) * upper).astype(jnp.bfloat16)
+    hidden = lax.optimization_barrier((jax.nn.silu(gate) * upper).astype(jnp.bfloat16))
     ffn_part = lax.psum_scatter(
         jnp.dot(hidden, w_down, preferred_element_type=jnp.float32).astype(jnp.bfloat16),
         "tensor",

time: 295 us -> 297 us (level)
  no operation moved by 1% of the time
where the time goes in v7:
time: 297 us; the launch traced here: 296 us
  waiting for transfers between devices  169 us (57%)
  blocking collectives  45.8 us (15%)
  matrix products  25.1 us (8%)
  local copies, waits for them, and re-layouts  18.4 us (6%)
  other arithmetic  15.5 us (5%)
  between operations  15 us (5%)
  starting transfers between devices  6.97 us (2%)
    reduce_scatter x1, waiting for transfers between devices, on_device(): lax.psum_scatter(jnp.dot(hidden, w_down, preferred_element_type=jnp.float...  59.2 us
    all_gather x1, waiting for transfers between devices, on_device(): full = lax.all_gather(grouped, 'tensor', axis=1, tiled=True)  51.1 us
    all_to_all x1, blocking collectives, on_device(): lax.all_to_all(payload, 'dp', split_axis=0, concat_axis=0, tiled=True)  45.8 us
    all_gather x1, waiting for transfers between devices, on_device(): attended_full = lax.all_gather(attended, 'tensor', axis=1, tiled=True)  33.3 us
    all_to_all x1, waiting for transfers between devices, on_device(): lax.all_to_all(back.reshape(groups, MOST, unit_rows, feat_part), 'dp', sp...  15.4 us
    all_gather x1, waiting for transfers between devices, on_device(): w_out_full = lax.all_gather(w_out, 'tensor', axis=0, tiled=True)  9.52 us
    dot_general x1, matrix products, on_device(): jnp.dot(attended_full, w_out_full, preferred_element_type=jnp.float32)  7.54 us
    all_to_all x1, starting transfers between devices, on_device(): lax.all_to_all(back.reshape(groups, MOST, unit_rows, feat_part), 'dp', sp...  6.63 us
  transfers between devices with their start and end apart: 5, of which 5 were waited for; matrix products, arithmetic and copies ran while one was open for 6% of the time, Pallas kernels for 0%

profile of v7, /device:TPU:65, one launch (start us, length us, event | category | flops | bytes accessed | tf_op | source)
XLA Modules:
  0.0 296.1 jit_solution(13938295347407967790)
XLA Ops:
  10.2 2.6 gather_fusion
  12.9 1.3 fusion.25
  14.2 45.8 %all_to_all.10 = bf16[32,72,256]{2,1,0:T(8,128)(2,1)S(1)} all-to-all(bf16[32,72,256]{2,1,0:T(8,128)(2,1)S(1)} %fusion.25), channel_id=1, replica_groups=mesh['dp'=32,'tensor'=8] {'dp'}, dimensions={0} | all-to-all | bytes 2359296 | tf_op jit(solution)/shard_map/all_to_all | solution.py:97
  61.2 2.4 slice.142
  63.7 2.6 gather_fusion.1
  66.3 9.5 %all-gather.4.cloned.1.call-done = bf16[1024,2048]{1,0:T(8,128)(2,1)} async-done(((bf16[128,2048]{1,0:T(8,128)(2,1)}), bf16[1024,2048]{1,0:T(8,128)(2,1)}) %all-gather.4.cloned.1.call-update) | async-done | bytes 4194320 | tf_op jit(solution)/shard_map/all_gather | solution.py:86
  80.0 1.9 constant_dynamic-slice_fusion
  82.4 51.1 %all-gather.6.cloned.1.call-done = bf16[1024,2048]{1,0:T(8,128)(2,1)} async-done(((bf16[1024,256]{1,0:T(8,128)(2,1)}), bf16[1024,2048]{1,0:T(8,128)(2,1)}) %all-gather.6.cloned.1.call-update) | async-done | bytes 4194320 | tf_op jit(solution)/shard_map/all_gather | solution.py:106
  133.5 3.2 %fusion.3 = f32[1024]{0:T(1024)S(1)} fusion(bf16[1024,2048]{1,0:T(8,128)(2,1)} %all-gather.6.cloned.1.call-done), kind=kLoop, calls=%fused_computation.13 | loop fusion | flops 6290432 | bytes 4198400 | tf_op jit(solution)/shard_map/reduce_sum | solution.py:21
  137.0 2.7 fusion.11
  140.1 1.2 fusion.38
  142.2 1.1 fusion.18
  143.4 1.3 fusion.26
  146.4 33.3 %all-gather.8.cloned.1.call-done = bf16[1024,1024]{0,1:T(8,128)(2,1)} async-done(((bf16[1024,128]{0,1:T(8,128)(2,1)}), bf16[1024,1024]{0,1:T(8,128)(2,1)}) %all-gather.8.cloned.1.call-update) | async-done | bytes 2097168 | tf_op jit(solution)/shard_map/all_gather | solution.py:158
  179.7 7.5 %convolution_convert_fusion.1 = bf16[1024,2048]{1,0:T(8,128)(2,1)S(1)} fusion(bf16[1024,1024]{0,1:T(8,128)(2,1)} %all-gather.8.cloned.1.call-done, bf16[1024,2048]{1,0:T(8,128)(2,1)} %all-gather.4.cloned.1.call-done), kind=kOutput, calls=%fused_computation.29 | convolution fusion | flops 4297064448 | bytes 10485760 | tf_op jit(solution)/shard_map/dot_general | solution.py:159
  187.3 2.0 fusion
  189.8 5.7 %fusion.7 = f32[1024,1280]{1,0:T(8,128)S(1)} fusion(bf16[2048,640]{1,0:T(8,128)(2,1)S(1)} %copy-done.17, bf16[2048,640]{1,0:T(8,128)(2,1)S(1)} %copy-done.18, bf16[1024,2048]{1,0:T(8,128)(2,1)S(1)} %get-tuple-element.23, f32[2048]{0:T(1024)S(1)} %copy-done.20, f32[1024]{0:T(1024)S(1)} %add_rsqrt_fusion.1), kind=kOutput, calls=%fused_computation.17 | convolution fusion | flops 5387583488 | bytes 14692352 | tf_op jit(solution)/shard_map/dot_general | solution.py:164
  196.3 5.2 %convolution_convert_fusion = bf16[1024,2048]{1,0:T(8,128)(2,1)} fusion(bf16[1024,640]{1,0:T(8,128)(2,1)S(1)} %fusion.19, bf16[640,2048]{1,0:T(8,128)(2,1)S(1)} %copy-done), kind=kOutput, calls=%fused_computation.28 | convolution fusion | flops 2686451712 | bytes 8126464 | tf_op jit(solution)/shard_map/dot_general | solution.py:171
  201.7 59.2 %reduce-scatter.2.cloned.1.call-done = bf16[1024,256]{1,0:T(8,128)(2,1)} async-done(((bf16[1024,2048]{1,0:T(8,128)(2,1)}), bf16[1024,256]{1,0:T(8,128)(2,1)}) %reduce-scatter.2.cloned.1.call-update) | async-done | bytes 524304 | tf_op jit(solution)/shard_map/reduce_scatter | solution.py:170
  260.9 1.3 add_convert_fusion
  262.3 1.6 gather_fusion.2
  263.9 6.6 %all-to-all-start.1 = ((bf16[32,2,32,256]{3,2,1,0:T(8,128)(2,1)}), bf16[32,2,32,256]{3,2,1,0:T(8,128)(2,1)}, u32[]{:S(2)}, u32[]{:S(2)}) async-start(bf16[32,2,32,256]{3,2,1,0:T(8,128)(2,1)} %bitcast.152), calls=%async_computation.2 | async-start | bytes 2097152 | tf_op jit(solution)/shard_map/all_to_all | solution.py:179
  271.5 15.4 %all-to-all-done.1 = bf16[32,2,32,256]{3,2,1,0:T(8,128)(2,1)} async-done(((bf16[32,2,32,256]{3,2,1,0:T(8,128)(2,1)}), bf16[32,2,32,256]{3,2,1,0:T(8,128)(2,1)}, u32[]{:S(2)}, u32[]{:S(2)}) %all-to-all-start.1) | async-done | bytes 1048608 | tf_op jit(solution)/shard_map/all_to_all | solution.py:179
  287.0 2.6 gather_fusion.3
  (111 shorter events, 13.6 us)
Async XLA Ops:
  7.2 189.1 %copy-start = (bf16[640,2048]{1,0:T(8,128)(2,1)S(1)}, bf16[640,2048]{1,0:T(8,128)(2,1)}, u32[]{:S(2)}) copy-start(bf16[640,2048]{1,0:T(8,128)(2,1)} %param.29) | copy-start | bytes 7864324
  7.2 68.7 %all-gather.4.cloned.1.call-start = ((), (), s32[]{:S(2)}) async-start(), calls=%async_computation.3 | async-start | bytes 4718592 | tf_op jit(solution)/shard_map/all_gather | solution.py:86
  7.9 125.6 %all-gather.6.cloned.1.call-start = ((), (), s32[]{:S(2)}) async-start(), calls=%async_computation.4 | async-start | bytes 4718592 | tf_op jit(solution)/shard_map/all_gather | solution.py:106
  12.9 63.0 %copy-start.13 = (s32[1,1024]{1,0:T(1,128)S(1)}, s32[1,1024]{1,0:T(1,128)}, u32[]{:S(2)}) copy-start(s32[1,1024]{1,0:T(1,128)} %param.18) | copy-start | bytes 12292
  63.6 73.2 %copy-start.19 = (f32[2048]{0:T(1024)S(1)}, f32[2048]{0:T(1024)}, u32[]{:S(2)}) copy-start(f32[2048]{0:T(1024)} %param.20) | copy-start | bytes 24580
  75.9 103.9 %all-gather.8.cloned.1.call-start = ((), (), s32[]{:S(2)}) async-start(), calls=%async_computation.5 | async-start | bytes 2359296 | tf_op jit(solution)/shard_map/all_gather | solution.py:158
  77.6 62.1 %copy-start.14 = (f32[32]{0:T(128)}, f32[32]{0:T(128)S(1)}, u32[]{:S(2)}) copy-start(f32[32]{0:T(128)S(1)} %multiply_power_fusion) | copy-start | bytes 388
  133.5 3.4 %copy-start.1 = (bf16[1024,2048]{1,0:T(8,128)(2,1)S(1)}, bf16[1024,2048]{1,0:T(8,128)(2,1)}, u32[]{:S(2)}) copy-start(bf16[1024,2048]{1,0:T(8,128)(2,1)} %all-gather.6.cloned.1.call-done) | copy-start | bytes 12582916
  137.0 3.0 %copy-start.15 = (f32[64]{0:T(128)S(1)}, f32[64]{0:T(128)}, u32[]{:S(2)}) copy-start(f32[64]{0:T(128)} %param.24) | copy-start | bytes 772
  137.0 3.1 %copy-start.12 = (f32[1024]{0:T(1024)S(1)}, f32[1024]{0:T(1024)}, u32[]{:S(2)}) copy-start(f32[1024]{0:T(1024)} %copy-done.11) | copy-start | bytes 12292
  137.0 4.3 %copy-start.16 = (f32[64]{0:T(128)S(1)}, f32[64]{0:T(128)}, u32[]{:S(2)}) copy-start(f32[64]{0:T(128)} %param.23) | copy-start | bytes 772
  141.3 2.1 copy-start.7
  146.2 114.7 %reduce-scatter.2.cloned.1.call-start = ((), (), s32[]{:S(2)}) async-start(), calls=%async_computation.6 | async-start | bytes 4718592 | tf_op jit(solution)/shard_map/reduce_scatter | solution.py:170
  179.7 7.6 %copy-start.2 = (bf16[1024,2048]{1,0:T(8,128)(2,1)S(1)}, bf16[1024,2048]{1,0:T(8,128)(2,1)}, u32[]{:S(2)}) copy-start(bf16[1024,2048]{1,0:T(8,128)(2,1)} %all-gather.6.cloned.1.call-done) | copy-start | bytes 12582916
  187.3 2.5 copy-start.18
  187.3 2.5 copy-start.20
  189.3 6.2 %copy-start.3 = (bf16[1024,2048]{1,0:T(8,128)(2,1)}, bf16[1024,2048]{1,0:T(8,128)(2,1)S(1)}, u32[]{:S(2)}) copy-start(bf16[1024,2048]{1,0:T(8,128)(2,1)S(1)} %get-tuple-element.23) | copy-start | bytes 12582916
  201.5 69.0 %copy-start.21 = (s32[1,32]{1,0:T(1,128)S(1)}, s32[1,32]{1,0:T(1,128)}, u32[]{:S(2)}) copy-start(s32[1,32]{1,0:T(1,128)} %param.17) | copy-start | bytes 388
  201.5 69.0 %copy-start.24 = (s32[32]{0:T(128)S(1)}, s32[32]{0:T(128)}, u32[]{:S(2)}) copy-start(s32[32]{0:T(128)} %copy-done.23) | copy-start | bytes 388
  201.5 69.1 %copy-start.22 = (s32[1,8]{1,0:T(1,128)S(1)}, s32[1,8]{1,0:T(1,128)}, u32[]{:S(2)}) copy-start(s32[1,8]{1,0:T(1,128)} %param.19) | copy-start | bytes 100
  201.5 69.1 %copy-start.8 = (bf16[1024,1,32]{0,2,1:T(8,128)(2,1)S(1)}, bf16[1024,1,32]{0,2,1:T(8,128)(2,1)}, u32[]{:S(2)}) copy-start(bf16[1024,1,32]{0,2,1:T(8,128)(2,1)} %copy-done.7) | copy-start | bytes 196612
  201.5 69.1 %copy-start.10 = (bf16[1024,1,32]{0,2,1:T(8,128)(2,1)S(1)}, bf16[1024,1,32]{0,2,1:T(8,128)(2,1)}, u32[]{:S(2)}) copy-start(bf16[1024,1,32]{0,2,1:T(8,128)(2,1)} %copy-done.9) | copy-start | bytes 196612
  263.9 23.0 %all-to-all-start.1 = ((bf16[32,2,32,256]{3,2,1,0:T(8,128)(2,1)}), bf16[32,2,32,256]{3,2,1,0:T(8,128)(2,1)}, u32[]{:S(2)}, u32[]{:S(2)}) async-start(bf16[32,2,32,256]{3,2,1,0:T(8,128)(2,1)} %bitcast.152), calls=%async_computation.2 | async-start | bytes 2097152 | tf_op jit(solution)/shard_map/all_to_all | solution.py:179
  271.5 18.0 %copy-start.5 = (bf16[8,128,64]{1,2,0:T(8,128)(2,1)}, bf16[8,128,64]{1,2,0:T(8,128)(2,1)S(1)}, u32[]{:S(2)}) copy-start(bf16[8,128,64]{1,2,0:T(8,128)(2,1)S(1)} %scatter_fusion) | copy-start | bytes 393220
  (6 other events, 8.1 us)
Sparse Core Ops, SparseCore 0:
  9.8 65.9 all-gather.3
  78.2 55.2 all-gather.5
  146.3 33.3 all-gather.7
  201.7 59.1 reduce-scatter.1

commit v8 on v6

--- a/solution.py
+++ b/solution.py
@@ -13,7 +13,8 @@
 
 EPS = 1e-06
 THETA = 10000.0
-BLOCK_ROWS = 512
+BLOCK_ROWS = 256
+LONGEST = 512
 
 
 def rms_scale(values, gain):
@@ -134,24 +135,25 @@
     outputs = []
     for first in range(0, tok_grp, block):
         last = first + block
+        low = max(0, (first - LONGEST) // block * block)
         scores = (
             jnp.einsum(
                 "ikgd,jkd->kgij",
                 grouped_q[first:last],
-                keys[:last],
+                keys[low:last],
                 preferred_element_type=jnp.float32,
             )
             * scale
         )
         query_rows = index[first:last]
         allowed = jnp.logical_and(
-            query_rows[:, None] >= index[None, :last],
-            starts[first:last][:, None] <= index[None, :last],
+            query_rows[:, None] >= index[None, low:last],
+            starts[first:last][:, None] <= index[None, low:last],
         )
         weights = jnp.where(allowed, jnp.exp(scores), 0.0)
         probs = (weights / jnp.sum(weights, axis=-1, keepdims=True)).astype(jnp.bfloat16)
         mixed = jnp.einsum(
-            "kgij,jkd->ikgd", probs, values[:last], preferred_element_type=jnp.float32
+            "kgij,jkd->ikgd", probs, values[low:last], preferred_element_type=jnp.float32
         )
         outputs.append(mixed.astype(jnp.bfloat16).reshape(block, q_heads * HEAD))
     attended = jnp.concatenate(outputs, axis=0)

time: 295 us -> 293 us (level)
  no operation moved by 1% of the time
where the time goes in v8:
time: 293 us
  waiting for transfers between devices  169 us (58%)
  blocking collectives  46.1 us (16%)
  matrix products  25.4 us (9%)
  local copies, waits for them, and re-layouts  17 us (6%)
  between operations  15.1 us (5%)
  other arithmetic  13.3 us (5%)
  starting transfers between devices  6.97 us (2%)
    reduce_scatter x1, waiting for transfers between devices, on_device(): lax.psum_scatter(jnp.dot(hidden, w_down, preferred_element_type=jnp.float...  59.2 us
    all_gather x1, waiting for transfers between devices, on_device(): full = lax.all_gather(grouped, 'tensor', axis=1, tiled=True)  51.3 us
    all_to_all x1, blocking collectives, on_device(): lax.all_to_all(payload, 'dp', split_axis=0, concat_axis=0, tiled=True)  46.1 us
    all_gather x1, waiting for transfers between devices, on_device(): attended_full = lax.all_gather(attended, 'tensor', axis=1, tiled=True)  33.3 us
    all_to_all x1, waiting for transfers between devices, on_device(): lax.all_to_all(back.reshape(groups, MOST, unit_rows, feat_part), 'dp', sp...  15.4 us
    dot_general x1, matrix products, on_device(): jnp.dot(attended_full, w_out_full, preferred_element_type=jnp.float32)  9.41 us
    all_gather x1, waiting for transfers between devices, on_device(): w_out_full = lax.all_gather(w_out, 'tensor', axis=0, tiled=True)  9.24 us
    all_to_all x1, starting transfers between devices, on_device(): lax.all_to_all(back.reshape(groups, MOST, unit_rows, feat_part), 'dp', sp...  6.63 us
  transfers between devices with their start and end apart: 5, of which 5 were waited for; matrix products, arithmetic and copies ran while one was open for 6% of the time, Pallas kernels for 0%

profile of v8, /device:TPU:65, one launch (start us, length us, event | category | flops | bytes accessed | tf_op | source)
XLA Modules:
  0.0 292.9 jit_solution(14233388828429262219)
XLA Ops:
  10.3 2.6 gather_fusion
  12.9 1.3 fusion.27
  14.3 46.1 %all_to_all.10 = bf16[32,72,256]{2,1,0:T(8,128)(2,1)S(1)} all-to-all(bf16[32,72,256]{2,1,0:T(8,128)(2,1)S(1)} %fusion.27), channel_id=1, replica_groups=mesh['dp'=32,'tensor'=8] {'dp'}, dimensions={0} | all-to-all | bytes 2359296 | tf_op jit(solution)/shard_map/all_to_all | solution.py:98
  60.3 1.0 copy-done.1
  61.6 2.4 slice.218
  64.0 2.6 gather_fusion.1
  66.6 9.2 %all-gather.4.cloned.1.call-done = bf16[1024,2048]{1,0:T(8,128)(2,1)} async-done(((bf16[128,2048]{1,0:T(8,128)(2,1)}), bf16[1024,2048]{1,0:T(8,128)(2,1)}) %all-gather.4.cloned.1.call-update) | async-done | bytes 4194320 | tf_op jit(solution)/shard_map/all_gather | solution.py:87
  78.7 0.8 compare_and_fusion.2
  80.0 1.2 compare_and_fusion
  81.2 1.1 constant_dynamic-slice_fusion
  82.3 51.3 %all-gather.6.cloned.1.call-done = bf16[1024,2048]{1,0:T(8,128)(2,1)} async-done(((bf16[1024,256]{1,0:T(8,128)(2,1)}), bf16[1024,2048]{1,0:T(8,128)(2,1)}) %all-gather.6.cloned.1.call-update) | async-done | bytes 4194320 | tf_op jit(solution)/shard_map/all_gather | solution.py:107
  133.6 3.2 %fusion.3 = f32[1024]{0:T(1024)S(1)} fusion(bf16[1024,2048]{1,0:T(8,128)(2,1)} %all-gather.6.cloned.1.call-done), kind=kLoop, calls=%fused_computation.13 | loop fusion | flops 6290432 | bytes 4198400 | tf_op jit(solution)/shard_map/reduce_sum | solution.py:22
  137.0 2.6 fusion.11
  144.8 33.3 %all-gather.8.cloned.1.call-done = bf16[1024,1024]{0,1:T(8,128)(2,1)} async-done(((bf16[1024,128]{0,1:T(8,128)(2,1)}), bf16[1024,1024]{0,1:T(8,128)(2,1)}) %all-gather.8.cloned.1.call-update) | async-done | bytes 2097168 | tf_op jit(solution)/shard_map/all_gather | solution.py:160
  178.1 9.4 %fusion = (f32[1024]{0:T(1024)S(1)}, bf16[1024,2048]{1,0:T(8,128)(2,1)S(1)}) fusion(bf16[1024,1024]{0,1:T(8,128)(2,1)} %all-gather.8.cloned.1.call-done, bf16[1024,2048]{1,0:T(8,128)(2,1)} %all-gather.4.cloned.1.call-done, bf16[1024,2048]{1,0:T(8,128)(2,1)} %all-gather.6.cloned.1.call-done), kind=kOutput, calls=%fused_computation.10 | convolution fusion | flops 4307549184 | bytes 14684160 | tf_op jit(solution)/shard_map/dot_general | solution.py:161
  187.6 5.7 %fusion.7 = f32[1024,1280]{1,0:T(8,128)S(1)} fusion(bf16[2048,640]{1,0:T(8,128)(2,1)S(1)} %copy-done.20, bf16[2048,640]{1,0:T(8,128)(2,1)S(1)} %copy-done.21, bf16[1024,2048]{1,0:T(8,128)(2,1)S(1)} %get-tuple-element.45, f32[2048]{0:T(1024)S(1)} %copy-done.23, f32[1024]{0:T(1024)S(1)} %add_rsqrt_fusion.1), kind=kOutput, calls=%fused_computation.17 | convolution fusion | flops 5387583488 | bytes 14692352 | tf_op jit(solution)/shard_map/dot_general | solution.py:165
  193.3 5.1 %convolution_convert_fusion = bf16[1024,2048]{1,0:T(8,128)(2,1)} fusion(bf16[640,2048]{1,0:T(8,128)(2,1)S(1)} %copy-done, f32[1024,1280]{1,0:T(8,128)S(1)} %fusion.7), kind=kOutput, calls=%fused_computation.26 | convolution fusion | flops 2690383872 | bytes 12058624 | tf_op jit(solution)/shard_map/dot_general | solution.py:172
  198.5 59.2 %reduce-scatter.2.cloned.1.call-done = bf16[1024,256]{1,0:T(8,128)(2,1)} async-done(((bf16[1024,2048]{1,0:T(8,128)(2,1)}), bf16[1024,256]{1,0:T(8,128)(2,1)}) %reduce-scatter.2.cloned.1.call-update) | async-done | bytes 524304 | tf_op jit(solution)/shard_map/reduce_scatter | solution.py:171
  257.7 1.3 add_convert_fusion
  259.0 1.6 gather_fusion.2
  260.7 6.6 %all-to-all-start.1 = ((bf16[32,2,32,256]{3,2,1,0:T(8,128)(2,1)}), bf16[32,2,32,256]{3,2,1,0:T(8,128)(2,1)}, u32[]{:S(2)}, u32[]{:S(2)}) async-start(bf16[32,2,32,256]{3,2,1,0:T(8,128)(2,1)} %bitcast.187), calls=%async_computation.2 | async-start | bytes 2097152 | tf_op jit(solution)/shard_map/all_to_all | solution.py:180
  267.5 0.8 scatter_fusion
  268.3 15.4 %all-to-all-done.1 = bf16[32,2,32,256]{3,2,1,0:T(8,128)(2,1)} async-done(((bf16[32,2,32,256]{3,2,1,0:T(8,128)(2,1)}), bf16[32,2,32,256]{3,2,1,0:T(8,128)(2,1)}, u32[]{:S(2)}, u32[]{:S(2)}) %all-to-all-start.1) | async-done | bytes 1048608 | tf_op jit(solution)/shard_map/all_to_all | solution.py:180
  283.7 2.6 gather_fusion.3
  (126 shorter events, 11.4 us)
Async XLA Ops:
  7.2 186.1 %copy-start = (bf16[640,2048]{1,0:T(8,128)(2,1)S(1)}, bf16[640,2048]{1,0:T(8,128)(2,1)}, u32[]{:S(2)}) copy-start(bf16[640,2048]{1,0:T(8,128)(2,1)} %param.29) | copy-start | bytes 7864324
  7.2 68.7 %all-gather.4.cloned.1.call-start = ((), (), s32[]{:S(2)}) async-start(), calls=%async_computation.3 | async-start | bytes 4718592 | tf_op jit(solution)/shard_map/all_gather | solution.py:87
  7.9 125.7 %all-gather.6.cloned.1.call-start = ((), (), s32[]{:S(2)}) async-start(), calls=%async_computation.4 | async-start | bytes 4718592 | tf_op jit(solution)/shard_map/all_gather | solution.py:107
  14.3 61.8 %copy-start.15 = (s32[1,1024]{1,0:T(1,128)S(1)}, s32[1,1024]{1,0:T(1,128)}, u32[]{:S(2)}) copy-start(s32[1,1024]{1,0:T(1,128)} %param.18) | copy-start | bytes 12292
  75.9 102.2 %all-gather.8.cloned.1.call-start = ((), (), s32[]{:S(2)}) async-start(), calls=%async_computation.5 | async-start | bytes 2359296 | tf_op jit(solution)/shard_map/all_gather | solution.py:160
  77.7 2.3 copy-start.16
  77.9 1.6 copy-start.13
  81.2 55.6 %copy-start.22 = (f32[2048]{0:T(1024)S(1)}, f32[2048]{0:T(1024)}, u32[]{:S(2)}) copy-start(f32[2048]{0:T(1024)} %param.20) | copy-start | bytes 24580
  133.6 3.4 %copy-start.2 = (bf16[1024,2048]{1,0:T(8,128)(2,1)S(1)}, bf16[1024,2048]{1,0:T(8,128)(2,1)}, u32[]{:S(2)}) copy-start(bf16[1024,2048]{1,0:T(8,128)(2,1)} %all-gather.6.cloned.1.call-done) | copy-start | bytes 12582916
  137.0 2.8 copy-start.18
  139.7 1.7 copy-start.10
  140.3 1.5 copy-start.9
  144.6 43.0 %copy-start.23 = (f32[2048]{0:T(1024)S(1)}, f32[2048]{0:T(1024)}, u32[]{:S(2)}) copy-start(f32[2048]{0:T(1024)} %param.26) | copy-start | bytes 24580
  144.6 113.1 %reduce-scatter.2.cloned.1.call-start = ((), (), s32[]{:S(2)}) async-start(), calls=%async_computation.6 | async-start | bytes 4718592 | tf_op jit(solution)/shard_map/reduce_scatter | solution.py:171
  178.1 9.5 %copy-start.20 = (bf16[2048,640]{1,0:T(8,128)(2,1)S(1)}, bf16[2048,640]{1,0:T(8,128)(2,1)}, u32[]{:S(2)}) copy-start(bf16[2048,640]{1,0:T(8,128)(2,1)} %param.28) | copy-start | bytes 7864324
  178.1 9.5 %copy-start.21 = (bf16[2048,640]{1,0:T(8,128)(2,1)S(1)}, bf16[2048,640]{1,0:T(8,128)(2,1)}, u32[]{:S(2)}) copy-start(bf16[2048,640]{1,0:T(8,128)(2,1)} %param.27) | copy-start | bytes 7864324
  187.5 5.7 %copy-start.11 = (bf16[1024,2048]{1,0:T(8,128)(2,1)}, bf16[1024,2048]{1,0:T(8,128)(2,1)S(1)}, u32[]{:S(2)}) copy-start(bf16[1024,2048]{1,0:T(8,128)(2,1)S(1)} %get-tuple-element.45) | copy-start | bytes 12582916
  198.5 68.9 %copy-start.24 = (s32[1,32]{1,0:T(1,128)S(1)}, s32[1,32]{1,0:T(1,128)}, u32[]{:S(2)}) copy-start(s32[1,32]{1,0:T(1,128)} %param.17) | copy-start | bytes 388
  198.5 68.9 %copy-start.27 = (s32[32]{0:T(128)S(1)}, s32[32]{0:T(128)}, u32[]{:S(2)}) copy-start(s32[32]{0:T(128)} %copy-done.26) | copy-start | bytes 388
  198.5 68.9 %copy-start.25 = (s32[1,8]{1,0:T(1,128)S(1)}, s32[1,8]{1,0:T(1,128)}, u32[]{:S(2)}) copy-start(s32[1,8]{1,0:T(1,128)} %param.19) | copy-start | bytes 100
  198.5 68.9 %copy-start.5 = (bf16[1024,1,32]{0,2,1:T(8,128)(2,1)S(1)}, bf16[1024,1,32]{0,2,1:T(8,128)(2,1)}, u32[]{:S(2)}) copy-start(bf16[1024,1,32]{0,2,1:T(8,128)(2,1)} %copy-done.4) | copy-start | bytes 196612
  198.5 68.9 %copy-start.7 = (bf16[1024,1,32]{0,2,1:T(8,128)(2,1)S(1)}, bf16[1024,1,32]{0,2,1:T(8,128)(2,1)}, u32[]{:S(2)}) copy-start(bf16[1024,1,32]{0,2,1:T(8,128)(2,1)} %copy-done.6) | copy-start | bytes 196612
  260.7 23.0 %all-to-all-start.1 = ((bf16[32,2,32,256]{3,2,1,0:T(8,128)(2,1)}), bf16[32,2,32,256]{3,2,1,0:T(8,128)(2,1)}, u32[]{:S(2)}, u32[]{:S(2)}) async-start(bf16[32,2,32,256]{3,2,1,0:T(8,128)(2,1)} %bitcast.187), calls=%async_computation.2 | async-start | bytes 2097152 | tf_op jit(solution)/shard_map/all_to_all | solution.py:180
  268.3 18.0 %copy-start.3 = (bf16[8,128,64]{1,2,0:T(8,128)(2,1)}, bf16[8,128,64]{1,2,0:T(8,128)(2,1)S(1)}, u32[]{:S(2)}) copy-start(bf16[8,128,64]{1,2,0:T(8,128)(2,1)S(1)} %scatter_fusion) | copy-start | bytes 393220
  (9 other events, 9.8 us)
Sparse Core Ops, SparseCore 0:
  9.8 65.9 all-gather.3
  78.3 55.2 all-gather.5
  144.7 33.3 all-gather.7
  198.5 59.1 reduce-scatter.1

commit v9 on v8

--- a/solution.py
+++ b/solution.py
@@ -13,7 +13,7 @@
 
 EPS = 1e-06
 THETA = 10000.0
-BLOCK_ROWS = 256
+BLOCK_ROWS = 128
 LONGEST = 512
 
 

time: 293 us -> 294 us (level)
  waiting for transfers between devices: 169 us -> 166 us
  transfers between devices with their start and end apart: 5 -> 5, of which waited for: 5 -> 5; matrix products, arithmetic and copies ran while one was open for 6% -> 7% of each run, Pallas kernels for 0% -> 0%
where the time goes in v9:
time: 294 us
  waiting for transfers between devices  166 us (56%)
  blocking collectives  46.1 us (16%)
  matrix products  26.6 us (9%)
  local copies, waits for them, and re-layouts  17.5 us (6%)
  other arithmetic  15.2 us (5%)
  between operations  15.2 us (5%)
  starting transfers between devices  6.94 us (2%)
    reduce_scatter x1, waiting for transfers between devices, on_device(): lax.psum_scatter(jnp.dot(hidden, w_down, preferred_element_type=jnp.float...  59.3 us
    all_gather x1, waiting for transfers between devices, on_device(): full = lax.all_gather(grouped, 'tensor', axis=1, tiled=True)  48.5 us
    all_to_all x1, blocking collectives, on_device(): lax.all_to_all(payload, 'dp', split_axis=0, concat_axis=0, tiled=True)  46.1 us
    all_gather x1, waiting for transfers between devices, on_device(): attended_full = lax.all_gather(attended, 'tensor', axis=1, tiled=True)  33.3 us
    all_to_all x1, waiting for transfers between devices, on_device(): lax.all_to_all(back.reshape(groups, MOST, unit_rows, feat_part), 'dp', sp...  15.4 us
    dot_general x1, matrix products, on_device(): jnp.dot(attended_full, w_out_full, preferred_element_type=jnp.float32)  9.41 us
    all_gather x1, waiting for transfers between devices, on_device(): w_out_full = lax.all_gather(w_out, 'tensor', axis=0, tiled=True)  9.28 us
    all_to_all x1, starting transfers between devices, on_device(): lax.all_to_all(back.reshape(groups, MOST, unit_rows, feat_part), 'dp', sp...  6.61 us
  transfers between devices with their start and end apart: 5, of which 5 were waited for; matrix products, arithmetic and copies ran while one was open for 7% of the time, Pallas kernels for 0%

profile of v9, /device:TPU:65, one launch (start us, length us, event | category | flops | bytes accessed | tf_op | source)
XLA Modules:
  0.0 293.9 jit_solution(8071440779037245672)
XLA Ops:
  10.3 2.6 gather_fusion
  12.9 1.3 fusion.38
  14.3 46.1 %all_to_all.10 = bf16[32,72,256]{2,1,0:T(8,128)(2,1)S(1)} all-to-all(bf16[32,72,256]{2,1,0:T(8,128)(2,1)S(1)} %fusion.38), channel_id=1, replica_groups=mesh['dp'=32,'tensor'=8] {'dp'}, dimensions={0} | all-to-all | bytes 2359296 | tf_op jit(solution)/shard_map/all_to_all | solution.py:98
  60.3 1.0 copy-done.1
  61.5 2.4 slice.338
  64.0 2.6 gather_fusion.1
  66.6 9.3 %all-gather.4.cloned.1.call-done = bf16[1024,2048]{1,0:T(8,128)(2,1)} async-done(((bf16[128,2048]{1,0:T(8,128)(2,1)}), bf16[1024,2048]{1,0:T(8,128)(2,1)}) %all-gather.4.cloned.1.call-update) | async-done | bytes 4194320 | tf_op jit(solution)/shard_map/all_gather | solution.py:87
  81.0 0.9 compare_and_fusion
  81.9 0.9 compare_and_fusion.2
  82.8 1.2 multiply_cosine_fusion
  84.0 1.1 constant_dynamic-slice_fusion
  85.1 48.5 %all-gather.6.cloned.1.call-done = bf16[1024,2048]{1,0:T(8,128)(2,1)} async-done(((bf16[1024,256]{1,0:T(8,128)(2,1)}), bf16[1024,2048]{1,0:T(8,128)(2,1)}) %all-gather.6.cloned.1.call-update) | async-done | bytes 4194320 | tf_op jit(solution)/shard_map/all_gather | solution.py:107
  133.6 3.2 %fusion.3 = f32[1024]{0:T(1024)S(1)} fusion(bf16[1024,2048]{1,0:T(8,128)(2,1)} %all-gather.6.cloned.1.call-done), kind=kLoop, calls=%fused_computation.13 | loop fusion | flops 6290432 | bytes 4198400 | tf_op jit(solution)/shard_map/reduce_sum | solution.py:22
  137.0 2.6 fusion.11
  145.9 33.3 %all-gather.8.cloned.1.call-done = bf16[1024,1024]{0,1:T(8,128)(2,1)} async-done(((bf16[1024,128]{0,1:T(8,128)(2,1)}), bf16[1024,1024]{0,1:T(8,128)(2,1)}) %all-gather.8.cloned.1.call-update) | async-done | bytes 2097168 | tf_op jit(solution)/shard_map/all_gather | solution.py:160
  179.2 9.4 %fusion = (f32[1024]{0:T(1024)S(1)}, bf16[1024,2048]{1,0:T(8,128)(2,1)S(1)}) fusion(bf16[1024,1024]{0,1:T(8,128)(2,1)} %all-gather.8.cloned.1.call-done, bf16[1024,2048]{1,0:T(8,128)(2,1)} %all-gather.4.cloned.1.call-done, bf16[1024,2048]{1,0:T(8,128)(2,1)} %all-gather.6.cloned.1.call-done), kind=kOutput, calls=%fused_computation.10 | convolution fusion | flops 4307549184 | bytes 14684160 | tf_op jit(solution)/shard_map/dot_general | solution.py:161
  188.6 5.7 %fusion.7 = f32[1024,1280]{1,0:T(8,128)S(1)} fusion(bf16[2048,640]{1,0:T(8,128)(2,1)S(1)} %copy-done.22, bf16[2048,640]{1,0:T(8,128)(2,1)S(1)} %copy-done.23, bf16[1024,2048]{1,0:T(8,128)(2,1)S(1)} %get-tuple-element.57, f32[2048]{0:T(1024)S(1)} %copy-done.25, f32[1024]{0:T(1024)S(1)} %add_rsqrt_fusion.1), kind=kOutput, calls=%fused_computation.17 | convolution fusion | flops 5387583488 | bytes 14692352 | tf_op jit(solution)/shard_map/dot_general | solution.py:165
  194.3 5.1 %convolution_convert_fusion = bf16[1024,2048]{1,0:T(8,128)(2,1)} fusion(bf16[640,2048]{1,0:T(8,128)(2,1)S(1)} %copy-done, f32[1024,1280]{1,0:T(8,128)S(1)} %fusion.7), kind=kOutput, calls=%fused_computation.26 | convolution fusion | flops 2690383872 | bytes 12058624 | tf_op jit(solution)/shard_map/dot_general | solution.py:172
  199.6 59.3 %reduce-scatter.2.cloned.1.call-done = bf16[1024,256]{1,0:T(8,128)(2,1)} async-done(((bf16[1024,2048]{1,0:T(8,128)(2,1)}), bf16[1024,256]{1,0:T(8,128)(2,1)}) %reduce-scatter.2.cloned.1.call-update) | async-done | bytes 524304 | tf_op jit(solution)/shard_map/reduce_scatter | solution.py:171
  258.8 1.3 add_convert_fusion
  260.2 1.6 gather_fusion.2
  261.8 6.6 %all-to-all-start.1 = ((bf16[32,2,32,256]{3,2,1,0:T(8,128)(2,1)}), bf16[32,2,32,256]{3,2,1,0:T(8,128)(2,1)}, u32[]{:S(2)}, u32[]{:S(2)}) async-start(bf16[32,2,32,256]{3,2,1,0:T(8,128)(2,1)} %bitcast.299), calls=%async_computation.2 | async-start | bytes 2097152 | tf_op jit(solution)/shard_map/all_to_all | solution.py:180
  269.4 15.4 %all-to-all-done.1 = bf16[32,2,32,256]{3,2,1,0:T(8,128)(2,1)} async-done(((bf16[32,2,32,256]{3,2,1,0:T(8,128)(2,1)}), bf16[32,2,32,256]{3,2,1,0:T(8,128)(2,1)}, u32[]{:S(2)}, u32[]{:S(2)}) %all-to-all-start.1) | async-done | bytes 1048608 | tf_op jit(solution)/shard_map/all_to_all | solution.py:180
  284.8 2.6 gather_fusion.3
  (160 shorter events, 14.8 us)
Async XLA Ops:
  7.2 187.2 %copy-start = (bf16[640,2048]{1,0:T(8,128)(2,1)S(1)}, bf16[640,2048]{1,0:T(8,128)(2,1)}, u32[]{:S(2)}) copy-start(bf16[640,2048]{1,0:T(8,128)(2,1)} %param.29) | copy-start | bytes 7864324
  7.2 68.7 %all-gather.4.cloned.1.call-start = ((), (), s32[]{:S(2)}) async-start(), calls=%async_computation.3 | async-start | bytes 4718592 | tf_op jit(solution)/shard_map/all_gather | solution.py:87
  7.9 125.7 %all-gather.6.cloned.1.call-start = ((), (), s32[]{:S(2)}) async-start(), calls=%async_computation.4 | async-start | bytes 4718592 | tf_op jit(solution)/shard_map/all_gather | solution.py:107
  12.9 63.3 %copy-start.17 = (s32[1,1024]{1,0:T(1,128)S(1)}, s32[1,1024]{1,0:T(1,128)}, u32[]{:S(2)}) copy-start(s32[1,1024]{1,0:T(1,128)} %param.18) | copy-start | bytes 12292
  63.9 72.9 %copy-start.24 = (f32[2048]{0:T(1024)S(1)}, f32[2048]{0:T(1024)}, u32[]{:S(2)}) copy-start(f32[2048]{0:T(1024)} %param.20) | copy-start | bytes 24580
  75.9 103.3 %all-gather.8.cloned.1.call-start = ((), (), s32[]{:S(2)}) async-start(), calls=%async_computation.5 | async-start | bytes 2359296 | tf_op jit(solution)/shard_map/all_gather | solution.py:160
  77.9 4.9 %copy-start.18 = (f32[32]{0:T(128)}, f32[32]{0:T(128)S(1)}, u32[]{:S(2)}) copy-start(f32[32]{0:T(128)S(1)} %multiply_power_fusion) | copy-start | bytes 388
  78.1 4.7 %copy-start.15 = (f32[1024]{0:T(1024)}, f32[1024]{0:T(1024)S(1)}, u32[]{:S(2)}) copy-start(f32[1024]{0:T(1024)S(1)} %get-tuple-element.22) | copy-start | bytes 12292
  133.6 3.4 %copy-start.2 = (bf16[1024,2048]{1,0:T(8,128)(2,1)S(1)}, bf16[1024,2048]{1,0:T(8,128)(2,1)}, u32[]{:S(2)}) copy-start(bf16[1024,2048]{1,0:T(8,128)(2,1)} %all-gather.6.cloned.1.call-done) | copy-start | bytes 12582916
  137.0 2.9 copy-start.20
  137.0 3.0 %copy-start.16 = (f32[1024]{0:T(1024)S(1)}, f32[1024]{0:T(1024)}, u32[]{:S(2)}) copy-start(f32[1024]{0:T(1024)} %copy-done.15) | copy-start | bytes 12292
  137.0 3.0 %copy-start.19 = (f32[32]{0:T(128)S(1)}, f32[32]{0:T(128)}, u32[]{:S(2)}) copy-start(f32[32]{0:T(128)} %copy-done.18) | copy-start | bytes 388
  137.0 3.6 %copy-start.21 = (f32[64]{0:T(128)S(1)}, f32[64]{0:T(128)}, u32[]{:S(2)}) copy-start(f32[64]{0:T(128)} %param.23) | copy-start | bytes 772
  139.8 2.6 copy-start.10
  145.7 42.9 %copy-start.25 = (f32[2048]{0:T(1024)S(1)}, f32[2048]{0:T(1024)}, u32[]{:S(2)}) copy-start(f32[2048]{0:T(1024)} %param.26) | copy-start | bytes 24580
  145.7 113.1 %reduce-scatter.2.cloned.1.call-start = ((), (), s32[]{:S(2)}) async-start(), calls=%async_computation.6 | async-start | bytes 4718592 | tf_op jit(solution)/shard_map/reduce_scatter | solution.py:171
  179.2 9.4 %copy-start.22 = (bf16[2048,640]{1,0:T(8,128)(2,1)S(1)}, bf16[2048,640]{1,0:T(8,128)(2,1)}, u32[]{:S(2)}) copy-start(bf16[2048,640]{1,0:T(8,128)(2,1)} %param.28) | copy-start | bytes 7864324
  179.2 9.5 %copy-start.23 = (bf16[2048,640]{1,0:T(8,128)(2,1)S(1)}, bf16[2048,640]{1,0:T(8,128)(2,1)}, u32[]{:S(2)}) copy-start(bf16[2048,640]{1,0:T(8,128)(2,1)} %param.27) | copy-start | bytes 7864324
  188.6 5.7 %copy-start.13 = (bf16[1024,2048]{1,0:T(8,128)(2,1)}, bf16[1024,2048]{1,0:T(8,128)(2,1)S(1)}, u32[]{:S(2)}) copy-start(bf16[1024,2048]{1,0:T(8,128)(2,1)S(1)} %get-tuple-element.57) | copy-start | bytes 12582916
  199.4 69.0 %copy-start.26 = (s32[1,32]{1,0:T(1,128)S(1)}, s32[1,32]{1,0:T(1,128)}, u32[]{:S(2)}) copy-start(s32[1,32]{1,0:T(1,128)} %param.17) | copy-start | bytes 388
  199.4 69.0 %copy-start.29 = (s32[32]{0:T(128)S(1)}, s32[32]{0:T(128)}, u32[]{:S(2)}) copy-start(s32[32]{0:T(128)} %copy-done.28) | copy-start | bytes 388
  199.4 69.1 %copy-start.27 = (s32[1,8]{1,0:T(1,128)S(1)}, s32[1,8]{1,0:T(1,128)}, u32[]{:S(2)}) copy-start(s32[1,8]{1,0:T(1,128)} %param.19) | copy-start | bytes 100
  261.8 23.0 %all-to-all-start.1 = ((bf16[32,2,32,256]{3,2,1,0:T(8,128)(2,1)}), bf16[32,2,32,256]{3,2,1,0:T(8,128)(2,1)}, u32[]{:S(2)}, u32[]{:S(2)}) async-start(bf16[32,2,32,256]{3,2,1,0:T(8,128)(2,1)} %bitcast.299), calls=%async_computation.2 | async-start | bytes 2097152 | tf_op jit(solution)/shard_map/all_to_all | solution.py:180
  269.4 18.0 %copy-start.3 = (bf16[8,128,64]{1,2,0:T(8,128)(2,1)}, bf16[8,128,64]{1,2,0:T(8,128)(2,1)S(1)}, u32[]{:S(2)}) copy-start(bf16[8,128,64]{1,2,0:T(8,128)(2,1)S(1)} %scatter_fusion) | copy-start | bytes 393220
  (11 other events, 17.1 us)
Sparse Core Ops, SparseCore 0:
  9.8 65.9 all-gather.3
  78.3 55.2 all-gather.5
  145.8 33.3 all-gather.7
  199.6 59.2 reduce-scatter.1
